TPU v7x, 128 devices: a whole 4x4x4 slice. The times are simulated.
128 devices in a mesh: entry: 4 (over y_hi, core), fft: 32 (over y_lo, z, x).
Axes of the slice: x: 4, y: 4 (y_hi: 2, y_lo: 2; y = y_hi * 2 + y_lo), z: 4, core: 2. Of those that a mesh axis runs over, the one named last changes fastest.
Arguments:
- left_zero_zero: int32 [2048, 4096], P('entry', 'fft'), may hold values from 0 to 65535
- left_zero_one: int32 [2048, 4096], P('entry', 'fft'), may hold values from 0 to 65535
- left_one_zero: int32 [2048, 4096], P('entry', 'fft'), may hold values from 0 to 65535
- left_one_one: int32 [2048, 4096], P('entry', 'fft'), may hold values from 0 to 65535
- right_zero_zero: int32 [2048, 4096], P('entry', 'fft'), may hold values from 0 to 65535
- right_zero_one: int32 [2048, 4096], P('entry', 'fft'), may hold values from 0 to 65535
- right_one_zero: int32 [2048, 4096], P('entry', 'fft'), may hold values from 0 to 65535
- right_one_one: int32 [2048, 4096], P('entry', 'fft'), may hold values from 0 to 65535
Outputs:
- product: float32 [4, 4096, 4096], P('entry', None, 'fft')
All inputs are finite; a program needn't handle non-finite values.
Results may differ from a plain program's by a relative error of at most 0.0001.
Values sent between devices are 32-bit elements; how exact they have to be, the bound alone decides.
No kernel may reach another device: no remote copies, remote signals or barrier semaphores. Data moves between devices by JAX's collectives and lax.ppermute only.
A program may use at most 128 MiB of HBM per device.

v0:
```python
import math

import jax
import jax.numpy as jnp
from jax import lax
from jax.sharding import PartitionSpec as P

RADIX = 64


exact_precision = lax.Precision.HIGHEST


def matmul(left_op, right_op):
    return jnp.dot(left_op, right_op, precision=exact_precision, preferred_element_type=jnp.float32)


def contract(pattern, left_op, right_op):
    return jnp.einsum(
        pattern, left_op, right_op, precision=exact_precision, preferred_element_type=jnp.float32
    )


def angle_table(first_part, second_part, length, sense_sign):
    turns = first_part[:, None] * second_part[None, :] % length
    phase_angle = turns.astype(jnp.float32) * (2.0 * math.pi / length)
    return (jnp.cos(phase_angle), sense_sign * jnp.sin(phase_angle))


def rotate(real_part, imag_part, cosine, sine):
    return (real_part * cosine - imag_part * sine, real_part * sine + imag_part * cosine)


def complex_product(left_real, left_imag, right_real, right_imag):
    return (
        left_real * right_real - left_imag * right_imag,
        left_real * right_imag + left_imag * right_real,
    )


def digits(limbs):
    return (limbs.astype(jnp.float32) - 32768.0) * (1.0 / 32768.0)


def column_transform(real_part, imag_part, length, radix_size, sense_sign, real_only):
    inner_size = length // radix_size
    outer_count = real_part.shape[0] // inner_size
    column_count = real_part.shape[1]
    first_cos, first_sin = angle_table(
        jnp.arange(radix_size, dtype=jnp.int32),
        jnp.arange(outer_count, dtype=jnp.int32),
        radix_size,
        sense_sign,
    )
    flat_real = real_part.reshape(outer_count, inner_size * column_count)
    step_real = matmul(first_cos, flat_real)
    step_imag = matmul(first_sin, flat_real)
    if imag_part is not None:
        flat_imag = imag_part.reshape(outer_count, inner_size * column_count)
        step_real = step_real - matmul(first_sin, flat_imag)
        step_imag = step_imag + matmul(first_cos, flat_imag)
    step_real = step_real.reshape(radix_size, inner_size, column_count)
    step_imag = step_imag.reshape(radix_size, inner_size, column_count)
    twist_cos, twist_sin = angle_table(
        jnp.arange(radix_size, dtype=jnp.int32),
        jnp.arange(inner_size, dtype=jnp.int32),
        length,
        sense_sign,
    )
    step_real, step_imag = rotate(
        step_real, step_imag, twist_cos[:, :, None], twist_sin[:, :, None]
    )
    second_cos, second_sin = angle_table(
        jnp.arange(inner_size, dtype=jnp.int32),
        jnp.arange(inner_size, dtype=jnp.int32),
        inner_size,
        sense_sign,
    )
    final_real = contract("mb,kbc->mkc", second_cos, step_real) - contract(
        "mb,kbc->mkc", second_sin, step_imag
    )
    final_real = final_real.reshape(length, column_count)
    if real_only:
        return final_real
    final_imag = contract("mb,kbc->mkc", second_sin, step_real) + contract(
        "mb,kbc->mkc", second_cos, step_imag
    )
    return (final_real, final_imag.reshape(length, column_count))


def row_transform(real_part, imag_part, length, radix_size, sense_sign):
    inner_size = length // radix_size
    row_count = real_part.shape[0]
    shaped_real = real_part.reshape(row_count, radix_size, inner_size)
    shaped_imag = imag_part.reshape(row_count, radix_size, inner_size)
    first_cos, first_sin = angle_table(
        jnp.arange(radix_size, dtype=jnp.int32),
        jnp.arange(radix_size, dtype=jnp.int32),
        radix_size,
        sense_sign,
    )
    step_real = contract("rab,ak->rkb", shaped_real, first_cos) - contract(
        "rab,ak->rkb", shaped_imag, first_sin
    )
    step_imag = contract("rab,ak->rkb", shaped_real, first_sin) + contract(
        "rab,ak->rkb", shaped_imag, first_cos
    )
    twist_cos, twist_sin = angle_table(
        jnp.arange(radix_size, dtype=jnp.int32),
        jnp.arange(inner_size, dtype=jnp.int32),
        length,
        sense_sign,
    )
    step_real, step_imag = rotate(step_real, step_imag, twist_cos[None], twist_sin[None])
    second_cos, second_sin = angle_table(
        jnp.arange(inner_size, dtype=jnp.int32),
        jnp.arange(inner_size, dtype=jnp.int32),
        inner_size,
        sense_sign,
    )
    final_real = contract("rkb,bm->rmk", step_real, second_cos) - contract(
        "rkb,bm->rmk", step_imag, second_sin
    )
    final_imag = contract("rkb,bm->rmk", step_real, second_sin) + contract(
        "rkb,bm->rmk", step_imag, second_cos
    )
    return (final_real.reshape(row_count, length), final_imag.reshape(row_count, length))


def local(
    left_zero_zero,
    left_zero_one,
    left_one_zero,
    left_one_one,
    right_zero_zero,
    right_zero_one,
    right_one_zero,
    right_one_one,
):
    lefts = [
        [digits(left_zero_zero), digits(left_zero_one)],
        [digits(left_one_zero), digits(left_one_one)],
    ]
    rights = [
        [digits(right_zero_zero), digits(right_zero_one)],
        [digits(right_one_zero), digits(right_one_one)],
    ]
    chosen = [
        [lefts[target // 2][0], lefts[target // 2][1], rights[0][target % 2], rights[1][target % 2]]
        for target in range(4)
    ]
    outgoing = jnp.stack([jnp.stack(member_list) for member_list in chosen], axis=1)
    arrived = lax.all_to_all(outgoing, "entry", split_axis=1, concat_axis=1, tiled=True)
    member_count = arrived.shape[0]
    local_cols = arrived.shape[3]
    arrived = arrived.reshape(member_count, -1, local_cols)
    row_count = 2 * arrived.shape[1]
    column_count = local_cols * lax.axis_size("fft")
    length = row_count * column_count
    fft_place = lax.axis_index("fft")
    global_cols = fft_place * local_cols + jnp.arange(local_cols, dtype=jnp.int32)
    twist_cos, twist_sin = angle_table(
        jnp.arange(row_count, dtype=jnp.int32), global_cols, length, -1.0
    )
    real_list = []
    imag_list = []
    for member in range(member_count):
        part_real, part_imag = column_transform(
            arrived[member], None, row_count, RADIX, -1.0, False
        )
        part_real, part_imag = rotate(part_real, part_imag, twist_cos, twist_sin)
        real_list.append(part_real)
        imag_list.append(part_imag)
    piece_real = lax.all_to_all(
        jnp.stack(real_list), "fft", split_axis=1, concat_axis=2, tiled=True
    )
    piece_imag = lax.all_to_all(
        jnp.stack(imag_list), "fft", split_axis=1, concat_axis=2, tiled=True
    )
    done_real = []
    done_imag = []
    for member in range(piece_real.shape[0]):
        out_real, out_imag = row_transform(
            piece_real[member], piece_imag[member], column_count, RADIX, -1.0
        )
        done_real.append(out_real)
        done_imag.append(out_imag)
    spec_real = jnp.stack(done_real)
    spec_imag = jnp.stack(done_imag)
    head_real, head_imag = complex_product(spec_real[0], spec_imag[0], spec_real[2], spec_imag[2])
    rest_real, rest_imag = complex_product(spec_real[1], spec_imag[1], spec_real[3], spec_imag[3])
    mixed_real = head_real + rest_real
    mixed_imag = head_imag + rest_imag
    mixed_real, mixed_imag = row_transform(mixed_real, mixed_imag, column_count, RADIX, 1.0)
    local_rows = mixed_real.shape[0]
    row_ids = fft_place * local_rows + jnp.arange(local_rows, dtype=jnp.int32)
    back_cos, back_sin = angle_table(
        row_ids, jnp.arange(column_count, dtype=jnp.int32), length, 1.0
    )
    mixed_real, mixed_imag = rotate(mixed_real, mixed_imag, back_cos, back_sin)
    full_real, full_imag = (
        lax.all_to_all(mixed_real, "fft", split_axis=1, concat_axis=0, tiled=True),
        lax.all_to_all(mixed_imag, "fft", split_axis=1, concat_axis=0, tiled=True),
    )
    values = column_transform(full_real, full_imag, row_count, RADIX, 1.0, True)
    out_scale = 1.0 / (length * math.sqrt(length // 2))
    return (values * out_scale)[None]


def solution(mesh):
    placed = (
        P("entry", "fft"),
        P("entry", "fft"),
        P("entry", "fft"),
        P("entry", "fft"),
        P("entry", "fft"),
        P("entry", "fft"),
        P("entry", "fft"),
        P("entry", "fft"),
    )
    return jax.shard_map(
        local, mesh=mesh, in_specs=placed, out_specs=P("entry", None, "fft"), check_vma=False
    )
```

profile of v0, /device:TPU:0, one launch (start us, length us, event | category | flops | bytes accessed | tf_op | source)
XLA Modules:
  0.0 693.2 jit_solution(7143584940309993605)
XLA Ops:
  5.2 4.8 all-to-all-start
  10.5 49.2 %all-to-all-done = f32[4,4,512,128]{3,2,0,1:T(8,128)} async-done(((f32[4,4,512,128]{3,2,0,1:T(8,128)}), f32[4,4,512,128]{3,2,0,1:T(8,128)}, u32[]{:S(2)}, u32[]{:S(2)}) %all-to-all-start) | async-done | bytes 4194336 | tf_op jit(solution)/shard_map/all_to_all | solution.py:153
  59.7 3.9 fusion.704
  65.7 3.3 fusion.229
  70.4 3.3 fusion.231
  73.7 3.3 fusion.233
  78.4 3.3 fusion.235
  81.7 3.3 fusion.237
  86.6 3.2 fusion.241
  89.8 7.0 %multiply_subtract_fusion.3 = (f32[64,64,128]{2,0,1:T(8,128)S(1)}, f32[64,64,128]{2,0,1:T(8,128)S(1)}, f32[64,64,128]{2,0,1:T(8,128)S(1)}, f32[64,64,128]{2,0,1:...) fusion(f32[64,64,128]{2,0,1:T(8,128)} %fusion.241, ...), kind=kOutput, calls=%fused_computation.92 | convolution fusion | flops 213940224 | bytes 32538624 | tf_op jit(solution)/shard_map/dot_general | solution.py:15
  106.1 3.5 fusion.105
  119.0 3.3 fusion.129
  144.3 3.6 fusion.152
  157.8 11.6 %fusion.24 = (f32[1,4096,128]{2,1,0:T(8,128)S(1)}, f32[1,4096,128]{2,1,0:T(8,128)S(1)}, f32[1,4096,128]{2,1,0:T(8,128)S(1)}, f32[1,4096,128]{2,1,0:T(8,128)}, f3...) fusion(s32[128]{0:T(128)S(1)} %iota_add_fusion, ...), kind=kLoop, calls=%fused_computation.59 | loop fusion | flops 20447232 | bytes 33554944 | tf_op jit(solution)/shard_map/sub | solution.py:31
  170.0 18.8 %copy.386 = f32[4,4096,128]{2,0,1:T(4,128)} copy(f32[4,4096,128]{2,1,0:T(8,128)S(1)} %pad_maximum_fusion.1) | data formatting | bytes 16777216 | tf_op jit(solution)/shard_map/stack | solution.py:178
  188.8 9.4 %all-to-all-start.2 = ((f32[4,4096,128]{2,0,1:T(4,128)}), f32[4,4096,128]{2,0,1:T(4,128)}, u32[]{:S(2)}, u32[]{:S(2)}) async-start(f32[4,4096,128]{2,0,1:T(4,128)} %copy.386), calls=%async_computation.2 | async-start | bytes 16777216 | tf_op jit(solution)/shard_map/all_to_all | solution.py:177
  201.3 18.7 %copy.381 = f32[4,4096,128]{2,0,1:T(4,128)} copy(f32[4,4096,128]{2,1,0:T(8,128)S(1)} %pad_maximum_fusion) | data formatting | bytes 16777216 | tf_op jit(solution)/shard_map/stack | solution.py:175
  220.1 90.4 %all-to-all-done.2 = f32[4,4096,128]{2,0,1:T(4,128)} async-done(((f32[4,4096,128]{2,0,1:T(4,128)}), f32[4,4096,128]{2,0,1:T(4,128)}, u32[]{:S(2)}, u32[]{:S(2)}) %all-to-all-start.2) | async-done | bytes 8388640 | tf_op jit(solution)/shard_map/all_to_all | solution.py:177
  310.5 17.7 %all-to-all-start.1 = ((f32[4,4096,128]{2,0,1:T(4,128)}), f32[4,4096,128]{2,0,1:T(4,128)}, u32[]{:S(2)}, u32[]{:S(2)}) async-start(f32[4,4096,128]{2,0,1:T(4,128)} %copy.381), calls=%async_computation.1 | async-start | bytes 16777216 | tf_op jit(solution)/shard_map/all_to_all | solution.py:174
  328.4 3.9 copy.387
  341.9 3.3 copy.404
  345.3 6.1 fusion.99
  351.4 4.5 fusion.97
  355.9 4.5 fusion.67
  360.5 4.7 fusion.65
  365.2 4.5 fusion.83
  369.7 4.5 fusion.81
  374.2 4.5 fusion.49
  378.7 4.9 fusion.51
  383.6 51.8 %all-to-all-done.1 = f32[4,4096,128]{2,0,1:T(4,128)} async-done(((f32[4,4096,128]{2,0,1:T(4,128)}), f32[4,4096,128]{2,0,1:T(4,128)}, u32[]{:S(2)}, u32[]{:S(2)}) %all-to-all-start.1) | async-done | bytes 8388640 | tf_op jit(solution)/shard_map/all_to_all | solution.py:174
  435.5 3.9 copy.382
  439.4 3.4 fusion.702
  444.7 6.2 fusion.161
  450.9 4.6 fusion.164
  460.4 6.8 fusion.185
  467.2 4.6 fusion.188
  474.9 6.8 fusion.173
  481.8 4.5 fusion.176
  486.3 4.6 fusion.200
  490.9 11.0 %subtract_bitcast_fusion.4 = (f32[128,64,64]{0,1,2:T(8,128)S(1)}, f32[128,64,64]{0,1,2:T(8,128)}, f32[128,64,64]{0,1,2:T(8,128)S(1)}, f32[128,64,64]{0,1,2:T(8,1...) fusion(f32[64,128,64]{1,0,2:T(8,128)} %fusion.176, ...), kind=kOutput, calls=%fused_computation.79 | convolution fusion | flops 415817728 | bytes 35684352 | tf_op jit(solution)/shard_map/rab,ak->rkb/dot_general | solution.py:19
  501.9 4.8 fusion.75
  513.0 3.6 fusion.89
  516.6 3.2 fusion.43
  526.1 3.4 fusion.57
  529.5 3.2 fusion.179
  532.7 3.2 fusion.182
  535.9 3.2 fusion.167
  539.1 3.4 fusion.170
  542.6 3.2 fusion.203
  545.8 3.2 fusion.206
  548.9 3.2 fusion.191
  552.1 5.2 subtract_add_fusion
  563.6 3.3 subtract_bitcast_fusion.1
  566.9 3.3 fusion.35
  573.4 3.2 subtract_bitcast_fusion
  577.8 3.4 add_bitcast_fusion
  582.5 10.0 %fusion.9 = (f32[128,32,128]{0,2,1:T(8,128)}, f32[128,32,128]{0,2,1:T(8,128)S(1)}) fusion(s32[32,128]{1,0:T(8,128)S(1)} %multiply_add_fusion.4, s32[128]{0:T(128)S(1)} %iota_add_fusion, f32[128,32,128]{0,2,1:T(8,128)S(1)} %bitcast.460, f32[128,32,128]{0,2,1:T(8,128)S(1)} %bitcast.459), kind=kLoop, calls=%fused_computation.28 | loop fusion | flops 10485760 | bytes 8405504 | tf_op jit(solution)/shard_map/add | solution.py:31
  592.5 47.4 %all_to_all.61 = f32[128,32,128]{0,2,1:T(8,128)S(1)} all-to-all(f32[128,32,128]{0,2,1:T(8,128)S(1)} %get-tuple-element.36), channel_id=1, replica_groups=mesh['entry'=4,'fft'=32] {'fft'}, dimensions={1} | all-to-all | bytes 4194304 | tf_op jit(solution)/shard_map/all_to_all | solution.py:202
  639.8 4.8 all-to-all-start.4
  648.2 3.5 fusion.369
  651.7 3.4 fusion.376
  655.1 16.6 %all-to-all-done.4 = f32[128,32,128]{0,2,1:T(8,128)} async-done(((f32[128,32,128]{0,2,1:T(8,128)}), f32[128,32,128]{0,2,1:T(8,128)}, u32[]{:S(2)}, u32[]{:S(2)}) %all-to-all-start.4) | async-done | bytes 2097184 | tf_op jit(solution)/shard_map/all_to_all | solution.py:203
  676.6 3.9 fusion.221
  687.0 3.2 subtract_multiply_fusion
  (100 shorter events, 127.8 us)
Async XLA Ops:
  0.0 2.3 copy-start.13
  0.0 2.3 copy-start.12
  0.0 2.4 copy-start.15
  0.0 2.4 copy-start.14
  5.2 54.5 %all-to-all-start = ((f32[4,4,512,128]{3,2,0,1:T(8,128)}), f32[4,4,512,128]{3,2,0,1:T(8,128)}, u32[]{:S(2)}, u32[]{:S(2)}) async-start(f32[4,4,512,128]{3,2,0,1:T(8,128)} %pad_maximum_fusion.2), calls=%async_computation | async-start | bytes 8388608 | tf_op jit(solution)/shard_map/all_to_all | solution.py:153
  188.8 121.7 %all-to-all-start.2 = ((f32[4,4096,128]{2,0,1:T(4,128)}), f32[4,4096,128]{2,0,1:T(4,128)}, u32[]{:S(2)}, u32[]{:S(2)}) async-start(f32[4,4096,128]{2,0,1:T(4,128)} %copy.386), calls=%async_computation.2 | async-start | bytes 16777216 | tf_op jit(solution)/shard_map/all_to_all | solution.py:177
  310.5 125.0 %all-to-all-start.1 = ((f32[4,4096,128]{2,0,1:T(4,128)}), f32[4,4096,128]{2,0,1:T(4,128)}, u32[]{:S(2)}, u32[]{:S(2)}) async-start(f32[4,4096,128]{2,0,1:T(4,128)} %copy.381), calls=%async_computation.1 | async-start | bytes 16777216 | tf_op jit(solution)/shard_map/all_to_all | solution.py:174
  345.3 6.2 copy-start.3
  351.4 4.5 copy-start.4
  360.5 4.7 copy-start.5
  444.7 6.2 copy-start.10
  460.4 6.9 copy-start
  460.4 6.9 copy-start.9
  474.9 6.9 copy-start.1
  474.9 6.9 copy-start.8
  481.8 4.5 copy-start.7
  501.9 4.9 copy-start.2
  545.7 3.2 copy-start.6
  639.8 31.9 %all-to-all-start.4 = ((f32[128,32,128]{0,2,1:T(8,128)}), f32[128,32,128]{0,2,1:T(8,128)}, u32[]{:S(2)}, u32[]{:S(2)}) async-start(f32[128,32,128]{0,2,1:T(8,128)} %get-tuple-element.35), calls=%async_computation.4 | async-start | bytes 4194304 | tf_op jit(solution)/shard_map/all_to_all | solution.py:203
  676.6 3.9 copy-start.11
where the time goes:
time: 703 us; the launch traced here: 693 us
  matrix products  264 us (38%)
  waiting for transfers between devices  208 us (30%)
  local copies, waits for them, and re-layouts  104 us (15%)
  blocking collectives  47.4 us (7%)
  starting transfers between devices  36.8 us (5%)
  other arithmetic  32 us (5%)
    dot_general x58, matrix products, contract(): jnp.einsum(pattern, left_op, right_op, precision=exact_precision, preferr...  223 us
    all_to_all x1, waiting for transfers between devices, local(): lax.all_to_all(jnp.stack(imag_list), 'fft', split_axis=1, concat_axis=2,...  90.4 us
    all_to_all x1, waiting for transfers between devices, local(): lax.all_to_all(jnp.stack(real_list), 'fft', split_axis=1, concat_axis=2,...  51.8 us
    all_to_all x1, waiting for transfers between devices, local(): lax.all_to_all(outgoing, 'entry', split_axis=1, concat_axis=1, tiled=True)  49.2 us
    all_to_all x1, blocking collectives, local(): lax.all_to_all(mixed_real, 'fft', split_axis=1, concat_axis=0, tiled=True)  47.4 us
    dot_general x12, matrix products, matmul(): jnp.dot(left_op, right_op, precision=exact_precision, preferred_element_t...  41.4 us
    another operation x1, local copies, waits for them, and re-layouts, local(): jnp.stack(imag_list)  18.8 us
    another operation x1, local copies, waits for them, and re-layouts, local(): jnp.stack(real_list)  18.7 us
  transfers between devices with their start and end apart: 4, of which 4 were waited for; matrix products, arithmetic and copies ran while one was open for 13% of the time, Pallas kernels for 0%

commit v1 on v0

v1 whole, which is shorter than its diff:
```python
import math

import jax
import jax.numpy as jnp
from jax import lax
from jax.sharding import PartitionSpec as P

RADIX = 64


exact_precision = lax.Precision.HIGHEST


def contract(pattern, left_op, right_op):
    return jnp.einsum(
        pattern, left_op, right_op, precision=exact_precision, preferred_element_type=jnp.float32
    )


def iota(count):
    return jnp.arange(count, dtype=jnp.int32)


def angle_table(first_part, second_part, length, sense_sign):
    turns = first_part[:, None] * second_part[None, :] % length
    phase_angle = turns.astype(jnp.float32) * (2.0 * math.pi / length)
    return (jnp.cos(phase_angle), sense_sign * jnp.sin(phase_angle))


def rotate(real_part, imag_part, cosine, sine):
    return (real_part * cosine - imag_part * sine, real_part * sine + imag_part * cosine)


def complex_product(left_real, left_imag, right_real, right_imag):
    return (
        left_real * right_real - left_imag * right_imag,
        left_real * right_imag + left_imag * right_real,
    )


def table_left(pattern, table, real_part, imag_part):
    cosine, sine = table
    if imag_part is None:
        return contract(pattern, cosine, real_part), contract(pattern, sine, real_part)
    return (
        contract(pattern, cosine, real_part) - contract(pattern, sine, imag_part),
        contract(pattern, sine, real_part) + contract(pattern, cosine, imag_part),
    )


def table_right(pattern, real_part, imag_part, table):
    cosine, sine = table
    return (
        contract(pattern, real_part, cosine) - contract(pattern, imag_part, sine),
        contract(pattern, real_part, sine) + contract(pattern, imag_part, cosine),
    )


def digits(limbs):
    return (limbs.astype(jnp.float32) - 32768.0) * (1.0 / 32768.0)


def column_half(values):
    row_count, column_count = values.shape
    length = 2 * row_count
    inner_size = length // RADIX
    outer_count = row_count // inner_size
    first = angle_table(iota(RADIX), iota(outer_count), RADIX, -1.0)
    flat = values.reshape(outer_count, inner_size * column_count)
    step_real, step_imag = table_left("ja,an->jn", first, flat, None)
    step_real = step_real.reshape(RADIX, inner_size, column_count)
    step_imag = step_imag.reshape(RADIX, inner_size, column_count)
    twist_cos, twist_sin = angle_table(iota(RADIX), iota(inner_size), length, -1.0)
    step_real, step_imag = rotate(
        step_real, step_imag, twist_cos[:, :, None], twist_sin[:, :, None]
    )
    second = angle_table(iota(inner_size // 2), iota(inner_size), inner_size, -1.0)
    final_real, final_imag = table_left("mb,jbc->mjc", second, step_real, step_imag)
    alternating = (1 - 2 * (iota(inner_size) % 2)).astype(jnp.float32)
    nyquist = contract("b,bc->c", alternating, step_real[0])
    final_imag = final_imag.at[0, 0].set(nyquist)
    return final_real, final_imag


def column_transform(real_part, imag_part, length, sense_sign):
    inner_size = length // RADIX
    outer_count = real_part.shape[0] // inner_size
    column_count = real_part.shape[1]
    first = angle_table(iota(RADIX), iota(outer_count), RADIX, sense_sign)
    flat_real = real_part.reshape(outer_count, inner_size * column_count)
    flat_imag = imag_part.reshape(outer_count, inner_size * column_count)
    step_real, step_imag = table_left("ja,an->jn", first, flat_real, flat_imag)
    step_real = step_real.reshape(RADIX, inner_size, column_count)
    step_imag = step_imag.reshape(RADIX, inner_size, column_count)
    twist_cos, twist_sin = angle_table(iota(RADIX), iota(inner_size), length, sense_sign)
    step_real, step_imag = rotate(
        step_real, step_imag, twist_cos[:, :, None], twist_sin[:, :, None]
    )
    second_cos, second_sin = angle_table(iota(inner_size), iota(inner_size), inner_size, sense_sign)
    final_real = contract("mb,kbc->mkc", second_cos, step_real) - contract(
        "mb,kbc->mkc", second_sin, step_imag
    )
    return final_real.reshape(length, column_count)


def row_forward(real_part, imag_part, sense_sign):
    source_count, _, column_count = real_part.shape
    length = source_count * column_count
    first = angle_table(iota(source_count), iota(source_count), source_count, sense_sign)
    step_real, step_imag = table_left("us,src->urc", first, real_part, imag_part)
    twist_cos, twist_sin = angle_table(iota(source_count), iota(column_count), length, sense_sign)
    step_real, step_imag = rotate(
        step_real, step_imag, twist_cos[:, None, :], twist_sin[:, None, :]
    )
    second = angle_table(iota(column_count), iota(column_count), column_count, sense_sign)
    return table_right("urc,cv->urv", step_real, step_imag, second)


def row_inverse(real_part, imag_part, sense_sign):
    source_count, _, column_count = real_part.shape
    length = source_count * column_count
    second = angle_table(iota(column_count), iota(column_count), column_count, sense_sign)
    step_real, step_imag = table_right("urv,vc->urc", real_part, imag_part, second)
    twist_cos, twist_sin = angle_table(iota(source_count), iota(column_count), length, sense_sign)
    step_real, step_imag = rotate(
        step_real, step_imag, twist_cos[:, None, :], twist_sin[:, None, :]
    )
    first = angle_table(iota(source_count), iota(source_count), source_count, sense_sign)
    return table_left("su,urc->src", first, step_real, step_imag)


def local(
    left_zero_zero,
    left_zero_one,
    left_one_zero,
    left_one_one,
    right_zero_zero,
    right_zero_one,
    right_one_zero,
    right_one_one,
):
    lefts = [[left_zero_zero, left_zero_one], [left_one_zero, left_one_one]]
    rights = [[right_zero_zero, right_zero_one], [right_one_zero, right_one_one]]
    entry_count = lax.axis_size("entry")
    fft_count = lax.axis_size("fft")
    fft_place = lax.axis_index("fft")
    on_first = fft_place == 0
    local_cols = left_zero_zero.shape[1]
    row_count = left_zero_zero.shape[0] * entry_count
    length = 2 * row_count * local_cols * fft_count
    column_count = local_cols * fft_count
    rows_here = 2 * row_count // (2 * fft_count)

    held_k1 = jnp.concatenate(
        [fft_place * rows_here + iota(rows_here), jnp.full((1,), row_count, jnp.int32)]
    )
    source_cols = (iota(fft_count)[:, None] * local_cols + iota(local_cols)[None, :])
    turns = source_cols[:, None, :] * held_k1[None, :, None] % length
    big_angle = turns.astype(jnp.float32) * (2.0 * math.pi / length)
    big_cos = jnp.cos(big_angle)
    big_sin = jnp.sin(big_angle)

    spectra = []
    for member in range(4):
        if member < 2:
            pieces = [lefts[target // 2][member] for target in range(4)]
        else:
            pieces = [rights[member - 2][target % 2] for target in range(4)]
        outgoing = digits(jnp.stack(pieces))
        arrived = lax.all_to_all(outgoing, "entry", 0, 0, tiled=True)
        arrived = arrived.reshape(row_count, local_cols)
        half_real, half_imag = column_half(arrived)
        payload = jnp.stack([half_real, half_imag], axis=1)
        got = lax.all_to_all(payload, "fft", 0, 0, tiled=True)
        got_real = got[:, 0]
        got_imag = got[:, 1]
        packed = got_imag[:, 0:1]
        nyquist_row = jnp.where(on_first, packed, 0.0)
        got_imag = jnp.concatenate(
            [jnp.where(on_first, 0.0, packed), got_imag[:, 1:], jnp.zeros_like(packed)], axis=1
        )
        got_real = jnp.concatenate([got_real, nyquist_row], axis=1)
        got_real, got_imag = rotate(got_real, got_imag, big_cos, -big_sin)
        spectra.append(row_forward(got_real, got_imag, -1.0))

    head_real, head_imag = complex_product(*spectra[0], *spectra[2])
    rest_real, rest_imag = complex_product(*spectra[1], *spectra[3])
    back_real, back_imag = row_inverse(head_real + rest_real, head_imag + rest_imag, 1.0)
    back_real, back_imag = rotate(back_real, back_imag, big_cos, big_sin)
    first_imag = jnp.where(on_first, back_real[:, rows_here:], back_imag[:, 0:1])
    back_imag = jnp.concatenate([first_imag, back_imag[:, 1:rows_here]], axis=1)
    back_real = back_real[:, :rows_here]
    payload = jnp.stack([back_real, back_imag], axis=1)
    got = lax.all_to_all(payload, "fft", 0, 0, tiled=True)
    full_real = got[:, 0].reshape(row_count, local_cols)
    full_imag = got[:, 1].reshape(row_count, local_cols)
    nyquist = full_imag[0]
    full_real = full_real.at[0].multiply(0.5)
    full_imag = full_imag.at[0].set(0.0)
    values = column_transform(full_real, full_imag, 2 * row_count, 1.0)
    alternating = (1 - 2 * (iota(2 * row_count) % 2)).astype(jnp.float32)
    values = 2.0 * values + alternating[:, None] * nyquist[None, :]
    out_scale = 1.0 / (length * math.sqrt(length // 2))
    return (values * out_scale)[None]


def solution(mesh):
    placed = (
        P("entry", "fft"),
        P("entry", "fft"),
        P("entry", "fft"),
        P("entry", "fft"),
        P("entry", "fft"),
        P("entry", "fft"),
        P("entry", "fft"),
        P("entry", "fft"),
    )
    return jax.shard_map(
        local, mesh=mesh, in_specs=placed, out_specs=P("entry", None, "fft"), check_vma=False
    )
```

time: 703 us -> 443 us (0.63)
  waiting for transfers between devices: 208 us -> 93.9 us
  local copies, waits for them, and re-layouts: 104 us -> 40.9 us
  blocking collectives: 47.4 us -> 0 us
  matrix products: 264 us -> 238 us
  other arithmetic: 32 us -> 11.5 us
  starting transfers between devices: 36.8 us -> 50.9 us
    all_to_all x4 -> x9, waiting for transfers between devices: 208 us -> 93.9 us  [the longest x5 55.1 us: local(): got = lax.all_to_all(payload, 'fft', 0, 0, tiled=True)]
    all_to_all x1 -> x0, blocking collectives: 47.4 us -> none  [local(): lax.all_to_all(mixed_real, 'fft', split_axis=1, concat_axis=0, tiled=True)]
    dot_general x12 -> x0, matrix products: 41.4 us -> none  [matmul(): jnp.dot(left_op, right_op, precision=exact_precision, preferred_element_t...]
    another operation x6 -> x12, local copies, waits for them, and re-layouts: 42.1 us -> 16.3 us  [the longest x4 10.3 us: local(): payload = jnp.stack([half_real, half_imag], axis=1)]
    slice x11 -> x14, local copies, waits for them, and re-layouts: 30 us -> 11.5 us  [the longest x4 6.87 us: local(): got_real = got[:, 0]]
    dot_general x58 -> x74, matrix products: 223 us -> 238 us  [contract(): jnp.einsum(pattern, left_op, right_op, precision=exact_precision, preferr...]
    all_to_all x4 -> x9, starting transfers between devices: 36.8 us -> 50.9 us  [the longest x5 33.7 us: local(): got = lax.all_to_all(payload, 'fft', 0, 0, tiled=True)]
    all_to_all x4 -> x0, local copies, waits for them, and re-layouts: 12.6 us -> none  [the longest x1 3.92 us: local(): lax.all_to_all(jnp.stack(imag_list), 'fft', split_axis=1, concat_axis=2,...]
  transfers between devices with their start and end apart: 4 -> 9, of which waited for: 4 -> 8; matrix products, arithmetic and copies ran while one was open for 13% -> 26% of each run, Pallas kernels for 0% -> 0%
where the time goes in v1:
time: 443 us; the launch traced here: 436 us
  matrix products  238 us (54%)
  waiting for transfers between devices  93.9 us (21%)
  starting transfers between devices  50.9 us (11%)
  local copies, waits for them, and re-layouts  40.9 us (9%)
  other arithmetic  11.5 us (3%)
    dot_general x74, matrix products, contract(): jnp.einsum(pattern, left_op, right_op, precision=exact_precision, preferr...  238 us
    all_to_all x5, waiting for transfers between devices, local(): got = lax.all_to_all(payload, 'fft', 0, 0, tiled=True)  55.1 us
    all_to_all x4, waiting for transfers between devices, local(): arrived = lax.all_to_all(outgoing, 'entry', 0, 0, tiled=True)  38.7 us
    all_to_all x5, starting transfers between devices, local(): got = lax.all_to_all(payload, 'fft', 0, 0, tiled=True)  33.7 us
    all_to_all x4, starting transfers between devices, local(): arrived = lax.all_to_all(outgoing, 'entry', 0, 0, tiled=True)  17.2 us
    another operation x4, local copies, waits for them, and re-layouts, local(): payload = jnp.stack([half_real, half_imag], axis=1)  10.3 us
  transfers between devices with their start and end apart: 9, of which 8 were waited for; matrix products, arithmetic and copies ran while one was open for 26% of the time, Pallas kernels for 0%

profile of v1, /device:TPU:0, one launch (start us, length us, event | category | flops | bytes accessed | tf_op | source)
XLA Modules:
  0.0 436.4 jit_solution(8720084396932329338)
XLA Ops:
  2.3 4.7 %all-to-all-start.6 = ((f32[4,512,128]{2,1,0:T(8,128)}), f32[4,512,128]{2,1,0:T(8,128)S(1)}, u32[]{:S(2)}, u32[]{:S(2)}) async-start(f32[4,512,128]{2,1,0:T(8,128)} %fusion.141), calls=%async_computation.6 | async-start | bytes 2097152 | tf_op jit(solution)/shard_map/all_to_all | solution.py:170
  8.1 14.9 %all-to-all-done.6 = f32[4,512,128]{2,1,0:T(8,128)S(1)} async-done(((f32[4,512,128]{2,1,0:T(8,128)}), f32[4,512,128]{2,1,0:T(8,128)S(1)}, u32[]{:S(2)}, u32[]{:S(2)}) %all-to-all-start.6) | async-done | bytes 1048608 | tf_op jit(solution)/shard_map/all_to_all | solution.py:170
  23.0 3.5 all-to-all-start.4
  29.3 13.1 %all-to-all-done.4 = f32[4,512,128]{2,1,0:T(8,128)S(1)} async-done(((f32[4,512,128]{2,1,0:T(8,128)}), f32[4,512,128]{2,1,0:T(8,128)S(1)}, u32[]{:S(2)}, u32[]{:S(2)}) %all-to-all-start.4) | async-done | bytes 1048608 | tf_op jit(solution)/shard_map/all_to_all | solution.py:170
  42.4 4.2 all-to-all-start
  46.9 3.3 fusion.118
  50.2 3.3 fusion.120
  53.4 3.2 fusion.122
  56.7 6.0 %all-to-all-done = f32[4,512,128]{2,1,0:T(8,128)} async-done(((f32[4,512,128]{2,1,0:T(8,128)}), f32[4,512,128]{2,1,0:T(8,128)}, u32[]{:S(2)}, u32[]{:S(2)}) %all-to-all-start) | async-done | bytes 1048608 | tf_op jit(solution)/shard_map/all_to_all | solution.py:170
  62.7 4.8 %all-to-all-start.2 = ((f32[4,512,128]{2,1,0:T(8,128)}), f32[4,512,128]{2,1,0:T(8,128)}, u32[]{:S(2)}, u32[]{:S(2)}) async-start(f32[4,512,128]{2,1,0:T(8,128)} %fusion.137), calls=%async_computation.2 | async-start | bytes 2097152 | tf_op jit(solution)/shard_map/all_to_all | solution.py:170
  68.9 3.2 fusion.124
  72.1 3.3 fusion.130
  75.4 3.3 fusion.132
  78.7 4.8 %all-to-all-done.2 = f32[4,512,128]{2,1,0:T(8,128)} async-done(((f32[4,512,128]{2,1,0:T(8,128)}), f32[4,512,128]{2,1,0:T(8,128)}, u32[]{:S(2)}, u32[]{:S(2)}) %all-to-all-start.2) | async-done | bytes 1048608 | tf_op jit(solution)/shard_map/all_to_all | solution.py:170
  86.8 8.7 %multiply_subtract_fusion.2 = (f32[64,64,128]{2,0,1:T(8,128)S(1)}, f32[64,64,128]{2,0,1:T(8,128)S(1)}, f32[64,64,128]{2,0,1:T(8,128)}, f32[64,64,128]{2,0,1:T(8,...) fusion(f32[64,64,128]{2,0,1:T(8,128)S(1)} %fusion.128, ...), kind=kOutput, calls=%fused_computation.29 | convolution fusion | flops 213940224 | bytes 32538624 | tf_op jit(solution)/shard_map/ja,an->jn/dot_general | solution.py:15
  100.3 2.4 fusion.64
  102.8 3.4 fusion.58
  107.6 2.6 copy.135
  110.3 8.6 %all-to-all-start.3 = ((f32[32,2,64,128]{3,2,1,0:T(8,128)}), f32[32,2,64,128]{3,2,1,0:T(8,128)}, u32[]{:S(2)}, u32[]{:S(2)}) async-start(f32[32,2,64,128]{3,2,1,0:T(8,128)} %copy.135), calls=%async_computation.3 | async-start | bytes 4194304 | tf_op jit(solution)/shard_map/all_to_all | solution.py:174
  120.0 4.0 fusion.7
  126.5 4.0 fusion.9
  130.5 2.4 fusion.82
  133.2 2.5 copy.163
  135.7 11.1 %all-to-all-done.3 = f32[32,2,64,128]{3,2,1,0:T(8,128)} async-done(((f32[32,2,64,128]{3,2,1,0:T(8,128)}), f32[32,2,64,128]{3,2,1,0:T(8,128)}, u32[]{:S(2)}, u32[]{:S(2)}) %all-to-all-start.3) | async-done | bytes 2097184 | tf_op jit(solution)/shard_map/all_to_all | solution.py:174
  146.9 5.8 %all-to-all-start.7 = ((f32[32,2,64,128]{3,2,1,0:T(8,128)}), f32[32,2,64,128]{3,2,1,0:T(8,128)}, u32[]{:S(2)}, u32[]{:S(2)}) async-start(f32[32,2,64,128]{3,2,1,0:T(8,128)} %copy.163), calls=%async_computation.7 | async-start | bytes 4194304 | tf_op jit(solution)/shard_map/all_to_all | solution.py:174
  154.1 4.0 fusion.15
  160.6 4.0 fusion.17
  164.7 2.4 fusion.70
  167.3 2.6 copy.151
  169.9 10.8 %all-to-all-done.7 = f32[32,2,64,128]{3,2,1,0:T(8,128)} async-done(((f32[32,2,64,128]{3,2,1,0:T(8,128)}), f32[32,2,64,128]{3,2,1,0:T(8,128)}, u32[]{:S(2)}, u32[]{:S(2)}) %all-to-all-start.7) | async-done | bytes 2097184 | tf_op jit(solution)/shard_map/all_to_all | solution.py:174
  180.7 5.4 %all-to-all-start.5 = ((f32[32,2,64,128]{3,2,1,0:T(8,128)}), f32[32,2,64,128]{3,2,1,0:T(8,128)}, u32[]{:S(2)}, u32[]{:S(2)}) async-start(f32[32,2,64,128]{3,2,1,0:T(8,128)} %copy.151), calls=%async_computation.5 | async-start | bytes 4194304 | tf_op jit(solution)/shard_map/all_to_all | solution.py:174
  186.2 3.9 fusion.31
  192.7 3.9 fusion.33
  196.6 2.4 fusion.46
  199.2 2.5 copy.123
  203.5 3.2 fusion.729
  208.9 5.5 %all-to-all-done.5 = f32[32,2,64,128]{3,2,1,0:T(8,128)} async-done(((f32[32,2,64,128]{3,2,1,0:T(8,128)}), f32[32,2,64,128]{3,2,1,0:T(8,128)}, u32[]{:S(2)}, u32[]{:S(2)}) %all-to-all-start.5) | async-done | bytes 2097184 | tf_op jit(solution)/shard_map/all_to_all | solution.py:174
  214.4 5.5 %all-to-all-start.1 = ((f32[32,2,64,128]{3,2,1,0:T(8,128)}), f32[32,2,64,128]{3,2,1,0:T(8,128)S(1)}, u32[]{:S(2)}, u32[]{:S(2)}) async-start(f32[32,2,64,128]{3,2,1,0:T(8,128)} %copy.123), calls=%async_computation.1 | async-start | bytes 4194304 | tf_op jit(solution)/shard_map/all_to_all | solution.py:174
  227.5 6.3 %fusion.295 = f32[32,65,128]{2,0,1:T(8,128)} fusion(f32[32,1,128]{2,0,1:T(8,128)S(1)} %get-tuple-element.114, f32[32,64,128]{2,0,1:T(8,128)S(1)} %bitcast.347, f32[32,1,128]{2,0,1:T(8,128)S(1)} %broadcast_in_dim.10, f32[32,63,128]{2,0,1:T(8,128)S(1)} %slice.240, f32[32,1,128]{2,0,1:T(8,128)S(1)} %get-tuple-element.113, s32[65]{0:T(128)S(1)} %pad_add_fusion, ...), kind=kOutput, calls=%fused_computation.358 | convolution fusion | flops 107841536 | bytes 3211524 | tf_op jit(solution)/shard_map/us,src->urc/dot_general | solution.py:15
  233.8 6.5 %fusion.298 = f32[32,65,128]{2,0,1:T(8,128)} fusion(f32[32,1,128]{2,0,1:T(8,128)S(1)} %get-tuple-element.116, f32[32,64,128]{2,0,1:T(8,128)S(1)} %bitcast.343, f32[32,1,128]{2,0,1:T(8,128)S(1)} %broadcast_in_dim.10, f32[32,63,128]{2,0,1:T(8,128)S(1)} %slice.235, f32[32,1,128]{2,0,1:T(8,128)S(1)} %get-tuple-element.115, s32[65]{0:T(128)S(1)} %pad_add_fusion, ...), kind=kOutput, calls=%fused_computation.361 | convolution fusion | flops 107841536 | bytes 3211524 | tf_op jit(solution)/shard_map/us,src->urc/dot_general | solution.py:15
  240.4 6.3 %fusion.256 = f32[32,65,128]{2,0,1:T(8,128)} fusion(f32[32,1,128]{2,0,1:T(8,128)S(1)} %get-tuple-element.114, f32[32,64,128]{2,0,1:T(8,128)S(1)} %bitcast.348, f32[32,1,128]{2,0,1:T(8,128)S(1)} %broadcast_in_dim.10, f32[32,63,128]{2,0,1:T(8,128)S(1)} %slice.240, f32[32,1,128]{2,0,1:T(8,128)S(1)} %get-tuple-element.113, s32[65]{0:T(128)S(1)} %pad_add_fusion, ...), kind=kOutput, calls=%fused_computation.319 | convolution fusion | flops 107842560 | bytes 3211524 | tf_op jit(solution)/shard_map/us,src->urc/dot_general | solution.py:15
  246.7 6.6 %fusion.259 = f32[32,65,128]{2,0,1:T(8,128)} fusion(f32[32,1,128]{2,0,1:T(8,128)S(1)} %get-tuple-element.116, f32[32,64,128]{2,0,1:T(8,128)S(1)} %bitcast.344, f32[32,1,128]{2,0,1:T(8,128)S(1)} %broadcast_in_dim.10, f32[32,63,128]{2,0,1:T(8,128)S(1)} %slice.235, f32[32,1,128]{2,0,1:T(8,128)S(1)} %get-tuple-element.115, s32[65]{0:T(128)S(1)} %pad_add_fusion, ...), kind=kOutput, calls=%fused_computation.322 | convolution fusion | flops 107842560 | bytes 3211524 | tf_op jit(solution)/shard_map/us,src->urc/dot_general | solution.py:15
  254.9 5.4 %fusion.304 = f32[32,65,128]{2,0,1:T(8,128)S(1)} fusion(f32[32,1,128]{2,0,1:T(8,128)S(1)} %get-tuple-element.112, f32[32,64,128]{2,0,1:T(8,128)S(1)} %bitcast.351, f32[32,1,128]{2,0,1:T(8,128)S(1)} %broadcast_in_dim.10, f32[32,63,128]{2,0,1:T(8,128)S(1)} %slice.225, f32[32,1,128]{2,0,1:T(8,128)S(1)} %get-tuple-element.111, s32[65]{0:T(128)S(1)} %pad_add_fusion, ...), kind=kOutput, calls=%fused_computation.367 | convolution fusion | flops 107841536 | bytes 3211524 | tf_op jit(solution)/shard_map/us,src->urc/dot_general | solution.py:15
  260.2 5.8 %fusion.265 = f32[32,65,128]{2,0,1:T(8,128)S(1)} fusion(f32[32,1,128]{2,0,1:T(8,128)S(1)} %get-tuple-element.112, f32[32,64,128]{2,0,1:T(8,128)S(1)} %bitcast.352, f32[32,1,128]{2,0,1:T(8,128)S(1)} %broadcast_in_dim.10, f32[32,63,128]{2,0,1:T(8,128)S(1)} %slice.225, f32[32,1,128]{2,0,1:T(8,128)S(1)} %get-tuple-element.111, s32[65]{0:T(128)S(1)} %pad_add_fusion, ...), kind=kOutput, calls=%fused_computation.328 | convolution fusion | flops 107842560 | bytes 3211524 | tf_op jit(solution)/shard_map/us,src->urc/dot_general | solution.py:15
  266.0 5.4 %fusion.262 = f32[32,65,128]{2,0,1:T(8,128)S(1)} fusion(f32[32,1,128]{2,0,1:T(8,128)S(1)} %get-tuple-element.110, f32[32,64,128]{2,0,1:T(8,128)S(1)} %get-tuple-element.130, f32[32,1,128]{2,0,1:T(8,128)S(1)} %broadcast_in_dim.10, f32[32,63,128]{2,0,1:T(8,128)S(1)} %copy-done.8, f32[32,1,128]{2,0,1:T(8,128)S(1)} %get-tuple-element.109, ...), kind=kOutput, calls=%fused_computation.325 | convolution fusion | flops 107842560 | bytes 3211524 | tf_op jit(solution)/shard_map/us,src->urc/dot_general | solution.py:15
  271.4 5.5 %fusion.301 = f32[32,65,128]{2,0,1:T(8,128)S(1)} fusion(f32[32,1,128]{2,0,1:T(8,128)S(1)} %get-tuple-element.110, f32[32,64,128]{2,0,1:T(8,128)S(1)} %get-tuple-element.130, f32[32,1,128]{2,0,1:T(8,128)S(1)} %broadcast_in_dim.10, f32[32,63,128]{2,0,1:T(8,128)S(1)} %copy-done.8, f32[32,1,128]{2,0,1:T(8,128)S(1)} %get-tuple-element.109, ...), kind=kOutput, calls=%fused_computation.364 | convolution fusion | flops 107841536 | bytes 3211524 | tf_op jit(solution)/shard_map/us,src->urc/dot_general | solution.py:15
  277.0 5.4 %convolution_subtract_fusion.7 = f32[32,65,128]{2,0,1:T(8,128)S(1)} fusion(f32[32,65,128]{2,0,1:T(8,128)S(1)} %copy-done.26, f32[32,1,128]{2,0,1:T(8,128)S(1)} %get-tuple-element.114, f32[32,64,128]{2,0,1:T(8,128)S(1)} %bitcast.349, f32[32,1,128]{2,0,1:T(8,128)S(1)} %broadcast_in_dim.10, f32[32,63,128]{2,0,1:T(8,128)S(1)} %copy-done.16, ...), kind=kOutput, calls=%fused_computation.84 | convolution fusion | flops 108108800 | bytes 4276484 | tf_op jit(solution)/shard_map/us,src->urc/dot_general | solution.py:15
  282.4 5.6 %convolution_add_fusion.7 = f32[32,65,128]{2,0,1:T(8,128)S(1)} fusion(f32[32,65,128]{2,0,1:T(8,128)S(1)} %copy-done.24, f32[32,1,128]{2,0,1:T(8,128)S(1)} %get-tuple-element.114, f32[32,64,128]{2,0,1:T(8,128)S(1)} %bitcast.350, f32[32,1,128]{2,0,1:T(8,128)S(1)} %broadcast_in_dim.10, f32[32,63,128]{2,0,1:T(8,128)S(1)} %copy-done.16, ...), kind=kOutput, calls=%fused_computation.83 | convolution fusion | flops 108107776 | bytes 4276484 | tf_op jit(solution)/shard_map/us,src->urc/dot_general | solution.py:15
  288.1 5.4 %convolution_subtract_fusion.8 = f32[32,65,128]{2,0,1:T(8,128)S(1)} fusion(f32[32,65,128]{2,0,1:T(8,128)S(1)} %copy-done.25, f32[32,1,128]{2,0,1:T(8,128)S(1)} %get-tuple-element.116, f32[32,64,128]{2,0,1:T(8,128)S(1)} %bitcast.345, f32[32,1,128]{2,0,1:T(8,128)S(1)} %broadcast_in_dim.10, f32[32,63,128]{2,0,1:T(8,128)S(1)} %copy-done.14, ...), kind=kOutput, calls=%fused_computation.86 | convolution fusion | flops 108108800 | bytes 4276484 | tf_op jit(solution)/shard_map/us,src->urc/dot_general | solution.py:15
  293.5 5.4 %convolution_add_fusion.8 = f32[32,65,128]{2,0,1:T(8,128)S(1)} fusion(f32[32,65,128]{2,0,1:T(8,128)S(1)} %copy-done.23, f32[32,1,128]{2,0,1:T(8,128)S(1)} %get-tuple-element.116, f32[32,64,128]{2,0,1:T(8,128)S(1)} %bitcast.346, f32[32,1,128]{2,0,1:T(8,128)S(1)} %broadcast_in_dim.10, f32[32,63,128]{2,0,1:T(8,128)S(1)} %copy-done.14, ...), kind=kOutput, calls=%fused_computation.85 | convolution fusion | flops 108107776 | bytes 4276484 | tf_op jit(solution)/shard_map/us,src->urc/dot_general | solution.py:15
  298.9 5.8 %convolution_subtract_fusion.10 = f32[32,65,128]{2,0,1:T(8,128)S(1)} fusion(f32[32,65,128]{2,0,1:T(8,128)S(1)} %fusion.304, f32[32,1,128]{2,0,1:T(8,128)S(1)} %get-tuple-element.112, f32[32,64,128]{2,0,1:T(8,128)S(1)} %bitcast.353, f32[32,1,128]{2,0,1:T(8,128)S(1)} %broadcast_in_dim.10, f32[32,63,128]{2,0,1:T(8,128)S(1)} %slice.225, ...), kind=kOutput, calls=%fused_computation.90 | convolution fusion | flops 108108800 | bytes 4276484 | tf_op jit(solution)/shard_map/us,src->urc/dot_general | solution.py:15
  304.7 5.4 %convolution_add_fusion.10 = f32[32,65,128]{2,0,1:T(8,128)S(1)} fusion(f32[32,65,128]{2,0,1:T(8,128)S(1)} %fusion.265, f32[32,1,128]{2,0,1:T(8,128)S(1)} %get-tuple-element.112, f32[32,64,128]{2,0,1:T(8,128)S(1)} %bitcast.354, f32[32,1,128]{2,0,1:T(8,128)S(1)} %broadcast_in_dim.10, f32[32,63,128]{2,0,1:T(8,128)S(1)} %slice.225, ...), kind=kOutput, calls=%fused_computation.89 | convolution fusion | flops 108107776 | bytes 4276484 | tf_op jit(solution)/shard_map/us,src->urc/dot_general | solution.py:15
  310.1 5.6 %convolution_subtract_fusion.9 = f32[32,65,128]{2,0,1:T(8,128)S(1)} fusion(f32[32,65,128]{2,0,1:T(8,128)S(1)} %fusion.301, f32[32,1,128]{2,0,1:T(8,128)S(1)} %get-tuple-element.110, f32[32,64,128]{2,0,1:T(8,128)S(1)} %get-tuple-element.130, f32[32,1,128]{2,0,1:T(8,128)S(1)} %broadcast_in_dim.10, f32[32,63,128]{2,0,1:T(8,128)S(1)} %copy-done.8, ...), kind=kOutput, calls=%fused_computation.88 | convolution fusion | flops 108108800 | bytes 4276484 | tf_op jit(solution)/shard_map/us,src->urc/dot_general | solution.py:15
  315.7 7.2 %multiply_add_fusion.10 = (f32[32,65,128]{2,0,1:T(8,128)S(1)}, f32[32,65,128]{2,0,1:T(8,128)S(1)}, f32[32,65,128]{2,0,1:T(8,128)S(1)}, f32[32,65,128]{2,0,1:T(8,...) fusion(f32[32,65,128]{2,0,1:T(8,128)S(1)} %convolution_subtract, ...), kind=kOutput, calls=%fused_computation.156 | convolution fusion | flops 114497536 | bytes 19218692 | tf_op jit(solution)/shard_map/us,src->urc/dot_general | solution.py:15
  335.1 2.4 fusion.101
  353.8 2.6 add_add_fusion
  365.1 5.5 %multiply_subtract_fusion.4 = (f32[32,65,128]{2,0,1:T(8,128)S(1)}, f32[32,65,128]{2,0,1:T(8,128)S(1)}) fusion(f32[32,65,128]{2,0,1:T(8,128)S(1)} %convolution_subtract_fusion.5, s32[65]{0:T(128)S(1)} %pad_add_fusion, s32[32,128]{1,0:T(8,128)S(1)} %iota_add_fusion, f32[32,65,128]{2,0,1:T(8,128)S(1)} %fusion.158, ...), kind=kOutput, calls=%fused_computation.145 | convolution fusion | flops 108640256 | bytes 6439172 | tf_op jit(solution)/shard_map/su,urc->src/dot_general | solution.py:15
  371.0 2.7 copy.176
  373.7 8.3 %all-to-all-start.8 = ((f32[32,2,64,128]{3,2,1,0:T(8,128)}), f32[32,2,64,128]{3,2,1,0:T(8,128)S(1)}, u32[]{:S(2)}, u32[]{:S(2)}) async-start(f32[32,2,64,128]{3,2,1,0:T(8,128)} %copy.176), calls=%async_computation.8 | async-start | bytes 4194304 | tf_op jit(solution)/shard_map/all_to_all | solution.py:194
  382.3 27.7 %all-to-all-done.8 = f32[32,2,64,128]{3,2,1,0:T(8,128)S(1)} async-done(((f32[32,2,64,128]{3,2,1,0:T(8,128)}), f32[32,2,64,128]{3,2,1,0:T(8,128)S(1)}, u32[]{:S(2)}, u32[]{:S(2)}) %all-to-all-start.8) | async-done | bytes 2097184 | tf_op jit(solution)/shard_map/all_to_all | solution.py:194
  411.4 3.2 fusion.387
  419.9 3.6 fusion.41
  426.7 3.1 fusion.3
  429.8 3.4 subtract_multiply_fusion
  (156 shorter events, 91.4 us)
Async XLA Ops:
  2.3 4.7 %copy-start.17 = (s32[512,128]{1,0:T(8,128)S(1)}, s32[512,128]{1,0:T(8,128)}, u32[]{:S(2)}) copy-start(s32[512,128]{1,0:T(8,128)} %param.23) | copy-start | bytes 786436
  2.3 4.7 %copy-start.18 = (s32[512,128]{1,0:T(8,128)S(1)}, s32[512,128]{1,0:T(8,128)}, u32[]{:S(2)}) copy-start(s32[512,128]{1,0:T(8,128)} %param.21) | copy-start | bytes 786436
  2.3 20.6 %all-to-all-start.6 = ((f32[4,512,128]{2,1,0:T(8,128)}), f32[4,512,128]{2,1,0:T(8,128)S(1)}, u32[]{:S(2)}, u32[]{:S(2)}) async-start(f32[4,512,128]{2,1,0:T(8,128)} %fusion.141), calls=%async_computation.6 | async-start | bytes 2097152 | tf_op jit(solution)/shard_map/all_to_all | solution.py:170
  8.1 18.9 %copy-start.19 = (s32[512,128]{1,0:T(8,128)S(1)}, s32[512,128]{1,0:T(8,128)}, u32[]{:S(2)}) copy-start(s32[512,128]{1,0:T(8,128)} %param.25) | copy-start | bytes 786436
  8.1 18.9 %copy-start.20 = (s32[512,128]{1,0:T(8,128)S(1)}, s32[512,128]{1,0:T(8,128)}, u32[]{:S(2)}) copy-start(s32[512,128]{1,0:T(8,128)} %param.24) | copy-start | bytes 786436
  23.0 19.4 %all-to-all-start.4 = ((f32[4,512,128]{2,1,0:T(8,128)}), f32[4,512,128]{2,1,0:T(8,128)S(1)}, u32[]{:S(2)}, u32[]{:S(2)}) async-start(f32[4,512,128]{2,1,0:T(8,128)} %fusion.139), calls=%async_computation.4 | async-start | bytes 2097152 | tf_op jit(solution)/shard_map/all_to_all | solution.py:170
  26.5 1.5 copy-start.21
  26.5 1.5 copy-start.22
  42.4 20.2 %all-to-all-start = ((f32[4,512,128]{2,1,0:T(8,128)}), f32[4,512,128]{2,1,0:T(8,128)}, u32[]{:S(2)}, u32[]{:S(2)}) async-start(f32[4,512,128]{2,1,0:T(8,128)} %fusion.135), calls=%async_computation | async-start | bytes 2097152 | tf_op jit(solution)/shard_map/all_to_all | solution.py:170
  62.7 20.8 %all-to-all-start.2 = ((f32[4,512,128]{2,1,0:T(8,128)}), f32[4,512,128]{2,1,0:T(8,128)}, u32[]{:S(2)}, u32[]{:S(2)}) async-start(f32[4,512,128]{2,1,0:T(8,128)} %fusion.137), calls=%async_computation.2 | async-start | bytes 2097152 | tf_op jit(solution)/shard_map/all_to_all | solution.py:170
  84.8 1.9 copy-start.4
  110.3 36.6 %all-to-all-start.3 = ((f32[32,2,64,128]{3,2,1,0:T(8,128)}), f32[32,2,64,128]{3,2,1,0:T(8,128)}, u32[]{:S(2)}, u32[]{:S(2)}) async-start(f32[32,2,64,128]{3,2,1,0:T(8,128)} %copy.135), calls=%async_computation.3 | async-start | bytes 4194304 | tf_op jit(solution)/shard_map/all_to_all | solution.py:174
  120.0 4.1 copy-start.2
  126.5 4.1 copy-start.3
  146.9 33.8 %all-to-all-start.7 = ((f32[32,2,64,128]{3,2,1,0:T(8,128)}), f32[32,2,64,128]{3,2,1,0:T(8,128)}, u32[]{:S(2)}, u32[]{:S(2)}) async-start(f32[32,2,64,128]{3,2,1,0:T(8,128)} %copy.163), calls=%async_computation.7 | async-start | bytes 4194304 | tf_op jit(solution)/shard_map/all_to_all | solution.py:174
  154.1 4.1 copy-start
  160.6 4.1 copy-start.1
  180.7 33.7 %all-to-all-start.5 = ((f32[32,2,64,128]{3,2,1,0:T(8,128)}), f32[32,2,64,128]{3,2,1,0:T(8,128)}, u32[]{:S(2)}, u32[]{:S(2)}) async-start(f32[32,2,64,128]{3,2,1,0:T(8,128)} %copy.151), calls=%async_computation.5 | async-start | bytes 4194304 | tf_op jit(solution)/shard_map/all_to_all | solution.py:174
  214.4 38.9 %all-to-all-start.1 = ((f32[32,2,64,128]{3,2,1,0:T(8,128)}), f32[32,2,64,128]{3,2,1,0:T(8,128)S(1)}, u32[]{:S(2)}, u32[]{:S(2)}) async-start(f32[32,2,64,128]{3,2,1,0:T(8,128)} %copy.123), calls=%async_computation.1 | async-start | bytes 4194304 | tf_op jit(solution)/shard_map/all_to_all | solution.py:174
  219.9 1.9 copy-start.5
  221.7 1.6 copy-start.7
  223.9 1.6 copy-start.6
  224.0 16.4 %copy-start.15 = (f32[32,63,128]{2,0,1:T(8,128)}, f32[32,63,128]{2,0,1:T(8,128)S(1)}, u32[]{:S(2)}) copy-start(f32[32,63,128]{2,0,1:T(8,128)S(1)} %slice.240) | copy-start | bytes 3096580
  226.1 14.3 %copy-start.11 = (f32[32,1,64,128]{3,0,2,1:T(8,128)}, f32[32,1,64,128]{3,0,2,1:T(8,128)S(1)}, u32[]{:S(2)}) copy-start(f32[32,1,64,128]{3,0,2,1:T(8,128)S(1)} %copy.368) | copy-start | bytes 3145732
  226.8 19.9 %copy-start.13 = (f32[32,63,128]{2,0,1:T(8,128)}, f32[32,63,128]{2,0,1:T(8,128)S(1)}, u32[]{:S(2)}) copy-start(f32[32,63,128]{2,0,1:T(8,128)S(1)} %slice.235) | copy-start | bytes 3096580
  227.4 19.3 %copy-start.9 = (f32[32,1,64,128]{3,0,2,1:T(8,128)}, f32[32,1,64,128]{3,0,2,1:T(8,128)S(1)}, u32[]{:S(2)}) copy-start(f32[32,1,64,128]{3,0,2,1:T(8,128)S(1)} %copy.370) | copy-start | bytes 3145732
  260.2 5.8 %copy-start.8 = (f32[32,63,128]{2,0,1:T(8,128)S(1)}, f32[32,63,128]{2,0,1:T(8,128)}, u32[]{:S(2)}) copy-start(f32[32,63,128]{2,0,1:T(8,128)} %slice.230) | copy-start | bytes 3096580
  271.4 5.6 %copy-start.12 = (f32[32,1,64,128]{3,0,2,1:T(8,128)S(1)}, f32[32,1,64,128]{3,0,2,1:T(8,128)}, u32[]{:S(2)}) copy-start(f32[32,1,64,128]{3,0,2,1:T(8,128)} %copy-done.11) | copy-start | bytes 3145732
  271.4 5.6 %copy-start.16 = (f32[32,63,128]{2,0,1:T(8,128)S(1)}, f32[32,63,128]{2,0,1:T(8,128)}, u32[]{:S(2)}) copy-start(f32[32,63,128]{2,0,1:T(8,128)} %copy-done.15) | copy-start | bytes 3096580
  271.4 5.6 %copy-start.26 = (f32[32,65,128]{2,0,1:T(8,128)S(1)}, f32[32,65,128]{2,0,1:T(8,128)}, u32[]{:S(2)}) copy-start(f32[32,65,128]{2,0,1:T(8,128)} %fusion.295) | copy-start | bytes 3194884
  277.0 5.4 %copy-start.24 = (f32[32,65,128]{2,0,1:T(8,128)S(1)}, f32[32,65,128]{2,0,1:T(8,128)}, u32[]{:S(2)}) copy-start(f32[32,65,128]{2,0,1:T(8,128)} %fusion.256) | copy-start | bytes 3194884
  282.4 5.6 %copy-start.10 = (f32[32,1,64,128]{3,0,2,1:T(8,128)S(1)}, f32[32,1,64,128]{3,0,2,1:T(8,128)}, u32[]{:S(2)}) copy-start(f32[32,1,64,128]{3,0,2,1:T(8,128)} %copy-done.9) | copy-start | bytes 3145732
  282.4 5.6 %copy-start.14 = (f32[32,63,128]{2,0,1:T(8,128)S(1)}, f32[32,63,128]{2,0,1:T(8,128)}, u32[]{:S(2)}) copy-start(f32[32,63,128]{2,0,1:T(8,128)} %copy-done.13) | copy-start | bytes 3096580
  282.4 5.6 %copy-start.25 = (f32[32,65,128]{2,0,1:T(8,128)S(1)}, f32[32,65,128]{2,0,1:T(8,128)}, u32[]{:S(2)}) copy-start(f32[32,65,128]{2,0,1:T(8,128)} %fusion.298) | copy-start | bytes 3194884
  288.1 5.4 %copy-start.23 = (f32[32,65,128]{2,0,1:T(8,128)S(1)}, f32[32,65,128]{2,0,1:T(8,128)}, u32[]{:S(2)}) copy-start(f32[32,65,128]{2,0,1:T(8,128)} %fusion.259) | copy-start | bytes 3194884
  373.7 36.2 %all-to-all-start.8 = ((f32[32,2,64,128]{3,2,1,0:T(8,128)}), f32[32,2,64,128]{3,2,1,0:T(8,128)S(1)}, u32[]{:S(2)}, u32[]{:S(2)}) async-start(f32[32,2,64,128]{3,2,1,0:T(8,128)} %copy.176), calls=%async_computation.8 | async-start | bytes 4194304 | tf_op jit(solution)/shard_map/all_to_all | solution.py:194

commit v2 on v1

--- a/solution.py
+++ b/solution.py
@@ -71,9 +71,9 @@
     step_real = step_real.reshape(RADIX, inner_size, column_count)
     step_imag = step_imag.reshape(RADIX, inner_size, column_count)
     twist_cos, twist_sin = angle_table(iota(RADIX), iota(inner_size), length, -1.0)
-    step_real, step_imag = rotate(
+    step_real, step_imag = lax.optimization_barrier(rotate(
         step_real, step_imag, twist_cos[:, :, None], twist_sin[:, :, None]
-    )
+    ))
     second = angle_table(iota(inner_size // 2), iota(inner_size), inner_size, -1.0)
     final_real, final_imag = table_left("mb,jbc->mjc", second, step_real, step_imag)
     alternating = (1 - 2 * (iota(inner_size) % 2)).astype(jnp.float32)
@@ -180,7 +180,9 @@
             [jnp.where(on_first, 0.0, packed), got_imag[:, 1:], jnp.zeros_like(packed)], axis=1
         )
         got_real = jnp.concatenate([got_real, nyquist_row], axis=1)
-        got_real, got_imag = rotate(got_real, got_imag, big_cos, -big_sin)
+        got_real, got_imag = lax.optimization_barrier(
+            rotate(got_real, got_imag, big_cos, -big_sin)
+        )
         spectra.append(row_forward(got_real, got_imag, -1.0))
 
     head_real, head_imag = complex_product(*spectra[0], *spectra[2])

time: 443 us -> 394 us (0.89)
  matrix products: 238 us -> 169 us
  other arithmetic: 11.5 us -> 33.6 us
    dot_general x74, matrix products: 238 us -> 169 us  [contract(): jnp.einsum(pattern, left_op, right_op, precision=exact_precision, preferr...]
    add x0 -> x4, other arithmetic: none -> 20.9 us  [rotate(): real_part * sine + imag_part * cosine]
    unnamed x60 -> x40, local copies, waits for them, and re-layouts: 5.75 us -> 0.83 us
  transfers between devices with their start and end apart: 9 -> 9, of which waited for: 8 -> 8; matrix products, arithmetic and copies ran while one was open for 26% -> 30% of each run, Pallas kernels for 0% -> 0%
where the time goes in v2:
time: 394 us; the launch traced here: 387 us
  matrix products  169 us (43%)
  waiting for transfers between devices  91 us (23%)
  starting transfers between devices  51.8 us (13%)
  local copies, waits for them, and re-layouts  39.9 us (10%)
  other arithmetic  33.6 us (9%)
    dot_general x74, matrix products, contract(): jnp.einsum(pattern, left_op, right_op, precision=exact_precision, preferr...  169 us
    all_to_all x5, waiting for transfers between devices, local(): got = lax.all_to_all(payload, 'fft', 0, 0, tiled=True)  52.2 us
    all_to_all x4, waiting for transfers between devices, local(): arrived = lax.all_to_all(outgoing, 'entry', 0, 0, tiled=True)  38.7 us
    all_to_all x5, starting transfers between devices, local(): got = lax.all_to_all(payload, 'fft', 0, 0, tiled=True)  34.9 us
    add x4, other arithmetic, rotate(): real_part * sine + imag_part * cosine  20.9 us
    all_to_all x4, starting transfers between devices, local(): arrived = lax.all_to_all(outgoing, 'entry', 0, 0, tiled=True)  16.9 us
    another operation x4, local copies, waits for them, and re-layouts, local(): payload = jnp.stack([half_real, half_imag], axis=1)  10.3 us
  transfers between devices with their start and end apart: 9, of which 8 were waited for; matrix products, arithmetic and copies ran while one was open for 30% of the time, Pallas kernels for 0%

profile of v2, /device:TPU:0, one launch (start us, length us, event | category | flops | bytes accessed | tf_op | source)
XLA Modules:
  0.0 387.3 jit_solution(17640210564430583199)
XLA Ops:
  0.0 2.4 fusion.141
  2.4 4.7 %all-to-all-start.6 = ((f32[4,512,128]{2,1,0:T(8,128)}), f32[4,512,128]{2,1,0:T(8,128)S(1)}, u32[]{:S(2)}, u32[]{:S(2)}) async-start(f32[4,512,128]{2,1,0:T(8,128)} %fusion.141), calls=%async_computation.6 | async-start | bytes 2097152 | tf_op jit(solution)/shard_map/all_to_all | solution.py:170
  8.2 14.8 %all-to-all-done.6 = f32[4,512,128]{2,1,0:T(8,128)S(1)} async-done(((f32[4,512,128]{2,1,0:T(8,128)}), f32[4,512,128]{2,1,0:T(8,128)S(1)}, u32[]{:S(2)}, u32[]{:S(2)}) %all-to-all-start.6) | async-done | bytes 1048608 | tf_op jit(solution)/shard_map/all_to_all | solution.py:170
  23.0 3.5 all-to-all-start.4
  29.3 13.1 %all-to-all-done.4 = f32[4,512,128]{2,1,0:T(8,128)S(1)} async-done(((f32[4,512,128]{2,1,0:T(8,128)}), f32[4,512,128]{2,1,0:T(8,128)S(1)}, u32[]{:S(2)}, u32[]{:S(2)}) %all-to-all-start.4) | async-done | bytes 1048608 | tf_op jit(solution)/shard_map/all_to_all | solution.py:170
  42.4 4.3 %all-to-all-start = ((f32[4,512,128]{2,1,0:T(8,128)}), f32[4,512,128]{2,1,0:T(8,128)}, u32[]{:S(2)}, u32[]{:S(2)}) async-start(f32[4,512,128]{2,1,0:T(8,128)} %fusion.135), calls=%async_computation | async-start | bytes 2097152 | tf_op jit(solution)/shard_map/all_to_all | solution.py:170
  46.9 3.3 fusion.118
  50.2 3.3 fusion.120
  53.5 3.3 fusion.122
  56.7 6.0 %all-to-all-done = f32[4,512,128]{2,1,0:T(8,128)} async-done(((f32[4,512,128]{2,1,0:T(8,128)}), f32[4,512,128]{2,1,0:T(8,128)}, u32[]{:S(2)}, u32[]{:S(2)}) %all-to-all-start) | async-done | bytes 1048608 | tf_op jit(solution)/shard_map/all_to_all | solution.py:170
  62.7 4.5 %all-to-all-start.2 = ((f32[4,512,128]{2,1,0:T(8,128)}), f32[4,512,128]{2,1,0:T(8,128)}, u32[]{:S(2)}, u32[]{:S(2)}) async-start(f32[4,512,128]{2,1,0:T(8,128)} %fusion.137), calls=%async_computation.2 | async-start | bytes 2097152 | tf_op jit(solution)/shard_map/all_to_all | solution.py:170
  68.6 3.3 fusion.124
  71.9 3.2 fusion.130
  75.1 3.2 fusion.132
  78.3 4.8 %all-to-all-done.2 = f32[4,512,128]{2,1,0:T(8,128)} async-done(((f32[4,512,128]{2,1,0:T(8,128)}), f32[4,512,128]{2,1,0:T(8,128)}, u32[]{:S(2)}, u32[]{:S(2)}) %all-to-all-start.2) | async-done | bytes 1048608 | tf_op jit(solution)/shard_map/all_to_all | solution.py:170
  86.5 8.7 %multiply_add_fusion.2 = (f32[64,64,128]{2,0,1:T(8,128)}, f32[64,64,128]{2,0,1:T(8,128)S(1)}, f32[64,64,128]{2,0,1:T(8,128)}, f32[64,64,128]{2,0,1:T(8,128)}, f3...) fusion(f32[64,64,128]{2,0,1:T(8,128)S(1)} %fusion.128, ...), kind=kOutput, calls=%fused_computation.28 | convolution fusion | flops 213940224 | bytes 32538624 | tf_op jit(solution)/shard_map/ja,an->jn/dot_general | solution.py:15
  95.2 2.4 fusion.7
  97.6 2.4 fusion.9
  100.0 2.4 fusion.88
  102.5 3.4 fusion.82
  107.4 2.6 copy.163
  110.0 8.6 %all-to-all-start.7 = ((f32[32,2,64,128]{3,2,1,0:T(8,128)}), f32[32,2,64,128]{3,2,1,0:T(8,128)}, u32[]{:S(2)}, u32[]{:S(2)}) async-start(f32[32,2,64,128]{3,2,1,0:T(8,128)} %copy.163), calls=%async_computation.7 | async-start | bytes 4194304 | tf_op jit(solution)/shard_map/all_to_all | solution.py:174
  120.1 4.0 %fusion.15 = f32[32,64,128]{2,0,1:T(8,128)S(1)} fusion(f32[64,64,128]{2,0,1:T(8,128)} %get-tuple-element.102), kind=kOutput, calls=%fused_computation.43 | convolution fusion | flops 201355264 | bytes 3145728 | tf_op jit(solution)/shard_map/mb,jbc->mjc/dot_general | solution.py:15
  124.1 2.4 fusion.76
  126.5 4.0 %fusion.17 = f32[32,64,128]{2,0,1:T(8,128)S(1)} fusion(f32[64,64,128]{2,0,1:T(8,128)} %get-tuple-element.102), kind=kOutput, calls=%fused_computation.45 | convolution fusion | flops 201357312 | bytes 3145728 | tf_op jit(solution)/shard_map/mb,jbc->mjc/dot_general | solution.py:15
  130.6 2.4 fusion.70
  133.3 2.5 copy.151
  135.8 10.8 %all-to-all-done.7 = f32[32,2,64,128]{3,2,1,0:T(8,128)} async-done(((f32[32,2,64,128]{3,2,1,0:T(8,128)}), f32[32,2,64,128]{3,2,1,0:T(8,128)}, u32[]{:S(2)}, u32[]{:S(2)}) %all-to-all-start.7) | async-done | bytes 2097184 | tf_op jit(solution)/shard_map/all_to_all | solution.py:174
  146.6 5.3 %all-to-all-start.5 = ((f32[32,2,64,128]{3,2,1,0:T(8,128)}), f32[32,2,64,128]{3,2,1,0:T(8,128)}, u32[]{:S(2)}, u32[]{:S(2)}) async-start(f32[32,2,64,128]{3,2,1,0:T(8,128)} %copy.151), calls=%async_computation.5 | async-start | bytes 4194304 | tf_op jit(solution)/shard_map/all_to_all | solution.py:174
  151.9 4.0 %fusion.31 = f32[32,64,128]{2,0,1:T(8,128)S(1)} fusion(f32[64,64,128]{2,0,1:T(8,128)} %get-tuple-element.94), kind=kOutput, calls=%fused_computation.59 | convolution fusion | flops 201355264 | bytes 3145728 | tf_op jit(solution)/shard_map/mb,jbc->mjc/dot_general | solution.py:15
  156.2 2.4 fusion.52
  159.0 4.0 %fusion.33 = f32[32,64,128]{2,0,1:T(8,128)S(1)} fusion(f32[64,64,128]{2,0,1:T(8,128)} %get-tuple-element.94), kind=kOutput, calls=%fused_computation.61 | convolution fusion | flops 201357312 | bytes 3145728 | tf_op jit(solution)/shard_map/mb,jbc->mjc/dot_general | solution.py:15
  163.1 2.4 fusion.46
  165.7 2.6 copy.123
  168.5 2.4 fusion.23
  170.9 3.3 fusion.64
  175.5 4.1 %fusion.25 = f32[32,64,128]{2,0,1:T(8,128)S(1)} fusion(f32[64,64,128]{2,0,1:T(8,128)} %get-tuple-element.98), kind=kOutput, calls=%fused_computation.53 | convolution fusion | flops 201357312 | bytes 3145728 | tf_op jit(solution)/shard_map/mb,jbc->mjc/dot_general | solution.py:15
  180.0 8.0 %all-to-all-start.1 = ((f32[32,2,64,128]{3,2,1,0:T(8,128)}), f32[32,2,64,128]{3,2,1,0:T(8,128)}, u32[]{:S(2)}, u32[]{:S(2)}) async-start(f32[32,2,64,128]{3,2,1,0:T(8,128)} %copy.123), calls=%async_computation.1 | async-start | bytes 4194304 | tf_op jit(solution)/shard_map/all_to_all | solution.py:174
  187.9 2.4 fusion.58
  191.9 2.5 copy.135
  202.3 13.6 %all-to-all-done.1 = f32[32,2,64,128]{3,2,1,0:T(8,128)} async-done(((f32[32,2,64,128]{3,2,1,0:T(8,128)}), f32[32,2,64,128]{3,2,1,0:T(8,128)}, u32[]{:S(2)}, u32[]{:S(2)}) %all-to-all-start.1) | async-done | bytes 2097184 | tf_op jit(solution)/shard_map/all_to_all | solution.py:174
  215.9 4.8 %all-to-all-start.3 = ((f32[32,2,64,128]{3,2,1,0:T(8,128)}), f32[32,2,64,128]{3,2,1,0:T(8,128)}, u32[]{:S(2)}, u32[]{:S(2)}) async-start(f32[32,2,64,128]{3,2,1,0:T(8,128)} %copy.135), calls=%async_computation.3 | async-start | bytes 4194304 | tf_op jit(solution)/shard_map/all_to_all | solution.py:174
  223.6 5.1 %multiply_add_fusion.7 = (f32[32,65,128]{2,0,1:T(8,128)S(1)}, f32[32,65,128]{2,0,1:T(8,128)S(1)}) fusion(f32[32,1,128]{2,0,1:T(8,128)S(1)} %get-tuple-element.154, f32[32,64,128]{2,0,1:T(8,128)S(1)} %get-tuple-element.176, f32[32,1,128]{2,0,1:T(8,128)S(1)} %broadcast_in_dim.10, f32[32,63,128]{2,0,1:T(8,128)S(1)} %copy-done.12, ...), kind=kLoop, calls=%fused_computation.150 | loop fusion | flops 6389760 | bytes 4276484 | tf_op jit(solution)/shard_map/add | solution.py:31
  228.7 5.1 %multiply_add_fusion.9 = (f32[32,65,128]{2,0,1:T(8,128)S(1)}, f32[32,65,128]{2,0,1:T(8,128)S(1)}) fusion(f32[32,1,128]{2,0,1:T(8,128)S(1)} %get-tuple-element.156, f32[32,64,128]{2,0,1:T(8,128)S(1)} %get-tuple-element.174, f32[32,1,128]{2,0,1:T(8,128)S(1)} %broadcast_in_dim.10, f32[32,63,128]{2,0,1:T(8,128)S(1)} %copy-done.13, ...), kind=kLoop, calls=%fused_computation.154 | loop fusion | flops 6389760 | bytes 4276484 | tf_op jit(solution)/shard_map/add | solution.py:31
  233.9 5.3 %multiply_add_fusion.13 = (f32[32,65,128]{2,0,1:T(8,128)S(1)}, f32[32,65,128]{2,0,1:T(8,128)S(1)}) fusion(f32[32,1,128]{2,0,1:T(8,128)S(1)} %get-tuple-element.152, f32[32,64,128]{2,0,1:T(8,128)S(1)} %get-tuple-element.172, f32[32,1,128]{2,0,1:T(8,128)S(1)} %broadcast_in_dim.10, f32[32,63,128]{2,0,1:T(8,128)S(1)} %slice.224, ...), kind=kLoop, calls=%fused_computation.162 | loop fusion | flops 6389760 | bytes 4276484 | tf_op jit(solution)/shard_map/add | solution.py:31
  239.2 2.2 fusion.295
  241.4 2.1 fusion.256
  243.4 2.1 fusion.298
  245.5 2.1 fusion.259
  247.7 2.1 fusion.304
  249.7 2.1 fusion.265
  254.8 5.5 %multiply_add_fusion.11 = (f32[32,65,128]{2,0,1:T(8,128)S(1)}, f32[32,65,128]{2,0,1:T(8,128)S(1)}) fusion(f32[32,1,128]{2,0,1:T(8,128)S(1)} %get-tuple-element.150, f32[32,64,128]{2,0,1:T(8,128)S(1)} %get-tuple-element.170, f32[32,1,128]{2,0,1:T(8,128)S(1)} %broadcast_in_dim.10, f32[32,63,128]{2,0,1:T(8,128)S(1)} %slice.228, ...), kind=kLoop, calls=%fused_computation.158 | loop fusion | flops 6389760 | bytes 4276484 | tf_op jit(solution)/shard_map/add | solution.py:31
  271.0 3.1 multiply_add_fusion.10
  284.1 2.2 fusion.95
  296.3 2.4 convolution_add_fusion.4
  304.9 2.6 add_add_fusion
  316.0 5.7 %multiply_subtract_fusion.4 = (f32[32,65,128]{2,0,1:T(8,128)S(1)}, f32[32,65,128]{2,0,1:T(8,128)S(1)}) fusion(f32[32,65,128]{2,0,1:T(8,128)S(1)} %convolution_subtract_fusion.5, s32[65]{0:T(128)S(1)} %pad_add_fusion, s32[32,128]{1,0:T(8,128)S(1)} %iota_add_fusion, f32[32,65,128]{2,0,1:T(8,128)S(1)} %fusion.158, ...), kind=kOutput, calls=%fused_computation.145 | convolution fusion | flops 108640256 | bytes 6439172 | tf_op jit(solution)/shard_map/su,urc->src/dot_general | solution.py:15
  322.2 2.5 copy.176
  324.7 8.2 %all-to-all-start.8 = ((f32[32,2,64,128]{3,2,1,0:T(8,128)}), f32[32,2,64,128]{3,2,1,0:T(8,128)S(1)}, u32[]{:S(2)}, u32[]{:S(2)}) async-start(f32[32,2,64,128]{3,2,1,0:T(8,128)} %copy.176), calls=%async_computation.8 | async-start | bytes 4194304 | tf_op jit(solution)/shard_map/all_to_all | solution.py:196
  333.2 27.4 %all-to-all-done.8 = f32[32,2,64,128]{3,2,1,0:T(8,128)S(1)} async-done(((f32[32,2,64,128]{3,2,1,0:T(8,128)}), f32[32,2,64,128]{3,2,1,0:T(8,128)S(1)}, u32[]{:S(2)}, u32[]{:S(2)}) %all-to-all-start.8) | async-done | bytes 2097184 | tf_op jit(solution)/shard_map/all_to_all | solution.py:196
  362.0 3.2 fusion.387
  370.6 3.6 fusion.41
  377.3 3.1 fusion.3
  380.4 3.5 subtract_multiply_fusion
  (143 shorter events, 88.7 us)
Async XLA Ops:
  2.4 4.7 %copy-start.14 = (s32[512,128]{1,0:T(8,128)S(1)}, s32[512,128]{1,0:T(8,128)}, u32[]{:S(2)}) copy-start(s32[512,128]{1,0:T(8,128)} %param.23) | copy-start | bytes 786436
  2.4 4.7 %copy-start.15 = (s32[512,128]{1,0:T(8,128)S(1)}, s32[512,128]{1,0:T(8,128)}, u32[]{:S(2)}) copy-start(s32[512,128]{1,0:T(8,128)} %param.21) | copy-start | bytes 786436
  2.4 20.6 %all-to-all-start.6 = ((f32[4,512,128]{2,1,0:T(8,128)}), f32[4,512,128]{2,1,0:T(8,128)S(1)}, u32[]{:S(2)}, u32[]{:S(2)}) async-start(f32[4,512,128]{2,1,0:T(8,128)} %fusion.141), calls=%async_computation.6 | async-start | bytes 2097152 | tf_op jit(solution)/shard_map/all_to_all | solution.py:170
  8.2 18.8 %copy-start.16 = (s32[512,128]{1,0:T(8,128)S(1)}, s32[512,128]{1,0:T(8,128)}, u32[]{:S(2)}) copy-start(s32[512,128]{1,0:T(8,128)} %param.25) | copy-start | bytes 786436
  8.2 18.9 %copy-start.17 = (s32[512,128]{1,0:T(8,128)S(1)}, s32[512,128]{1,0:T(8,128)}, u32[]{:S(2)}) copy-start(s32[512,128]{1,0:T(8,128)} %param.24) | copy-start | bytes 786436
  23.0 19.4 %all-to-all-start.4 = ((f32[4,512,128]{2,1,0:T(8,128)}), f32[4,512,128]{2,1,0:T(8,128)S(1)}, u32[]{:S(2)}, u32[]{:S(2)}) async-start(f32[4,512,128]{2,1,0:T(8,128)} %fusion.139), calls=%async_computation.4 | async-start | bytes 2097152 | tf_op jit(solution)/shard_map/all_to_all | solution.py:170
  26.5 1.5 copy-start.18
  26.6 1.5 copy-start.19
  42.4 20.3 %all-to-all-start = ((f32[4,512,128]{2,1,0:T(8,128)}), f32[4,512,128]{2,1,0:T(8,128)}, u32[]{:S(2)}, u32[]{:S(2)}) async-start(f32[4,512,128]{2,1,0:T(8,128)} %fusion.135), calls=%async_computation | async-start | bytes 2097152 | tf_op jit(solution)/shard_map/all_to_all | solution.py:170
  62.7 20.5 %all-to-all-start.2 = ((f32[4,512,128]{2,1,0:T(8,128)}), f32[4,512,128]{2,1,0:T(8,128)}, u32[]{:S(2)}, u32[]{:S(2)}) async-start(f32[4,512,128]{2,1,0:T(8,128)} %fusion.137), calls=%async_computation.2 | async-start | bytes 2097152 | tf_op jit(solution)/shard_map/all_to_all | solution.py:170
  84.6 1.9 copy-start.5
  110.0 36.6 %all-to-all-start.7 = ((f32[32,2,64,128]{3,2,1,0:T(8,128)}), f32[32,2,64,128]{3,2,1,0:T(8,128)}, u32[]{:S(2)}, u32[]{:S(2)}) async-start(f32[32,2,64,128]{3,2,1,0:T(8,128)} %copy.163), calls=%async_computation.7 | async-start | bytes 4194304 | tf_op jit(solution)/shard_map/all_to_all | solution.py:174
  120.1 4.1 %copy-start.2 = (f32[64,64,128]{2,0,1:T(8,128)S(1)}, f32[64,64,128]{2,0,1:T(8,128)}, u32[]{:S(2)}) copy-start(f32[64,64,128]{2,0,1:T(8,128)} %get-tuple-element.101) | copy-start | bytes 6291460
  126.5 4.1 %copy-start.3 = (f32[64,64,128]{2,0,1:T(8,128)S(1)}, f32[64,64,128]{2,0,1:T(8,128)}, u32[]{:S(2)}) copy-start(f32[64,64,128]{2,0,1:T(8,128)} %get-tuple-element.101) | copy-start | bytes 6291460
  146.6 33.4 %all-to-all-start.5 = ((f32[32,2,64,128]{3,2,1,0:T(8,128)}), f32[32,2,64,128]{3,2,1,0:T(8,128)}, u32[]{:S(2)}, u32[]{:S(2)}) async-start(f32[32,2,64,128]{3,2,1,0:T(8,128)} %copy.151), calls=%async_computation.5 | async-start | bytes 4194304 | tf_op jit(solution)/shard_map/all_to_all | solution.py:174
  151.9 4.1 %copy-start = (f32[64,64,128]{2,0,1:T(8,128)S(1)}, f32[64,64,128]{2,0,1:T(8,128)}, u32[]{:S(2)}) copy-start(f32[64,64,128]{2,0,1:T(8,128)} %get-tuple-element.93) | copy-start | bytes 6291460
  159.0 4.1 %copy-start.1 = (f32[64,64,128]{2,0,1:T(8,128)S(1)}, f32[64,64,128]{2,0,1:T(8,128)}, u32[]{:S(2)}) copy-start(f32[64,64,128]{2,0,1:T(8,128)} %get-tuple-element.93) | copy-start | bytes 6291460
  165.7 2.8 copy-start.4
  180.0 35.9 %all-to-all-start.1 = ((f32[32,2,64,128]{3,2,1,0:T(8,128)}), f32[32,2,64,128]{3,2,1,0:T(8,128)}, u32[]{:S(2)}, u32[]{:S(2)}) async-start(f32[32,2,64,128]{3,2,1,0:T(8,128)} %copy.123), calls=%async_computation.1 | async-start | bytes 4194304 | tf_op jit(solution)/shard_map/all_to_all | solution.py:174
  215.9 35.9 %all-to-all-start.3 = ((f32[32,2,64,128]{3,2,1,0:T(8,128)}), f32[32,2,64,128]{3,2,1,0:T(8,128)}, u32[]{:S(2)}, u32[]{:S(2)}) async-start(f32[32,2,64,128]{3,2,1,0:T(8,128)} %copy.135), calls=%async_computation.3 | async-start | bytes 4194304 | tf_op jit(solution)/shard_map/all_to_all | solution.py:174
  222.4 1.2 copy-start.12
  223.6 5.1 %copy-start.13 = (f32[32,63,128]{2,0,1:T(8,128)S(1)}, f32[32,63,128]{2,0,1:T(8,128)}, u32[]{:S(2)}) copy-start(f32[32,63,128]{2,0,1:T(8,128)} %slice.232) | copy-start | bytes 3096580
  261.4 1.2 copy-start.11
  262.6 1.2 copy-start.9
  263.9 1.2 copy-start.10
  265.1 1.2 copy-start.7
  266.3 1.2 copy-start.8
  267.6 1.2 copy-start.6
  324.7 35.9 %all-to-all-start.8 = ((f32[32,2,64,128]{3,2,1,0:T(8,128)}), f32[32,2,64,128]{3,2,1,0:T(8,128)S(1)}, u32[]{:S(2)}, u32[]{:S(2)}) async-start(f32[32,2,64,128]{3,2,1,0:T(8,128)} %copy.176), calls=%async_computation.8 | async-start | bytes 4194304 | tf_op jit(solution)/shard_map/all_to_all | solution.py:196

commit v3 on v2

--- a/solution.py
+++ b/solution.py
@@ -24,7 +24,7 @@
 def angle_table(first_part, second_part, length, sense_sign):
     turns = first_part[:, None] * second_part[None, :] % length
     phase_angle = turns.astype(jnp.float32) * (2.0 * math.pi / length)
-    return (jnp.cos(phase_angle), sense_sign * jnp.sin(phase_angle))
+    return lax.optimization_barrier((jnp.cos(phase_angle), sense_sign * jnp.sin(phase_angle)))
 
 
 def rotate(real_part, imag_part, cosine, sine):
@@ -82,21 +82,20 @@
     return final_real, final_imag
 
 
-def column_transform(real_part, imag_part, length, sense_sign):
+def column_part(real_part, imag_part, length, sense_sign, offset):
+    outer_count, part_size, column_count = real_part.shape
     inner_size = length // RADIX
-    outer_count = real_part.shape[0] // inner_size
-    column_count = real_part.shape[1]
     first = angle_table(iota(RADIX), iota(outer_count), RADIX, sense_sign)
-    flat_real = real_part.reshape(outer_count, inner_size * column_count)
-    flat_imag = imag_part.reshape(outer_count, inner_size * column_count)
+    flat_real = real_part.reshape(outer_count, part_size * column_count)
+    flat_imag = imag_part.reshape(outer_count, part_size * column_count)
     step_real, step_imag = table_left("ja,an->jn", first, flat_real, flat_imag)
-    step_real = step_real.reshape(RADIX, inner_size, column_count)
-    step_imag = step_imag.reshape(RADIX, inner_size, column_count)
-    twist_cos, twist_sin = angle_table(iota(RADIX), iota(inner_size), length, sense_sign)
-    step_real, step_imag = rotate(
+    step_real = step_real.reshape(RADIX, part_size, column_count)
+    step_imag = step_imag.reshape(RADIX, part_size, column_count)
+    twist_cos, twist_sin = angle_table(iota(RADIX), offset + iota(part_size), length, sense_sign)
+    step_real, step_imag = lax.optimization_barrier(rotate(
         step_real, step_imag, twist_cos[:, :, None], twist_sin[:, :, None]
-    )
-    second_cos, second_sin = angle_table(iota(inner_size), iota(inner_size), inner_size, sense_sign)
+    ))
+    second_cos, second_sin = angle_table(iota(inner_size), offset + iota(part_size), inner_size, sense_sign)
     final_real = contract("mb,kbc->mkc", second_cos, step_real) - contract(
         "mb,kbc->mkc", second_sin, step_imag
     )
@@ -157,8 +156,7 @@
     source_cols = (iota(fft_count)[:, None] * local_cols + iota(local_cols)[None, :])
     turns = source_cols[:, None, :] * held_k1[None, :, None] % length
     big_angle = turns.astype(jnp.float32) * (2.0 * math.pi / length)
-    big_cos = jnp.cos(big_angle)
-    big_sin = jnp.sin(big_angle)
+    big_cos, big_sin = lax.optimization_barrier((jnp.cos(big_angle), jnp.sin(big_angle)))
 
     spectra = []
     for member in range(4):
@@ -187,19 +185,41 @@
 
     head_real, head_imag = complex_product(*spectra[0], *spectra[2])
     rest_real, rest_imag = complex_product(*spectra[1], *spectra[3])
-    back_real, back_imag = row_inverse(head_real + rest_real, head_imag + rest_imag, 1.0)
-    back_real, back_imag = rotate(back_real, back_imag, big_cos, big_sin)
-    first_imag = jnp.where(on_first, back_real[:, rows_here:], back_imag[:, 0:1])
-    back_imag = jnp.concatenate([first_imag, back_imag[:, 1:rows_here]], axis=1)
-    back_real = back_real[:, :rows_here]
-    payload = jnp.stack([back_real, back_imag], axis=1)
-    got = lax.all_to_all(payload, "fft", 0, 0, tiled=True)
-    full_real = got[:, 0].reshape(row_count, local_cols)
-    full_imag = got[:, 1].reshape(row_count, local_cols)
-    nyquist = full_imag[0]
-    full_real = full_real.at[0].multiply(0.5)
-    full_imag = full_imag.at[0].set(0.0)
-    values = column_transform(full_real, full_imag, 2 * row_count, 1.0)
+    mixed_real = head_real + rest_real
+    mixed_imag = head_imag + rest_imag
+    part_rows = rows_here // 2
+    pieces = (
+        (slice(0, part_rows), True),
+        (slice(part_rows, rows_here), False),
+    )
+    values = None
+    nyquist = None
+    for rows, with_nyquist in pieces:
+        part_real = mixed_real[:, rows]
+        part_imag = mixed_imag[:, rows]
+        part_cos = big_cos[:, rows]
+        part_sin = big_sin[:, rows]
+        if with_nyquist:
+            part_real = jnp.concatenate([part_real, mixed_real[:, rows_here:]], axis=1)
+            part_imag = jnp.concatenate([part_imag, mixed_imag[:, rows_here:]], axis=1)
+            part_cos = jnp.concatenate([part_cos, big_cos[:, rows_here:]], axis=1)
+            part_sin = jnp.concatenate([part_sin, big_sin[:, rows_here:]], axis=1)
+        back_real, back_imag = row_inverse(part_real, part_imag, 1.0)
+        back_real, back_imag = rotate(back_real, back_imag, part_cos, part_sin)
+        if with_nyquist:
+            first_imag = jnp.where(on_first, back_real[:, part_rows:], back_imag[:, 0:1])
+            back_imag = jnp.concatenate([first_imag, back_imag[:, 1:part_rows]], axis=1)
+            back_real = back_real[:, :part_rows]
+        payload = jnp.stack([back_real, back_imag], axis=1)
+        got = lax.all_to_all(payload, "fft", 0, 0, tiled=True)
+        full_real = got[:, 0]
+        full_imag = got[:, 1]
+        if with_nyquist:
+            nyquist = full_imag[0, 0]
+            full_real = full_real.at[0, 0].multiply(0.5)
+            full_imag = full_imag.at[0, 0].set(0.0)
+        part = column_part(full_real, full_imag, 2 * row_count, 1.0, rows.start)
+        values = part if values is None else values + part
     alternating = (1 - 2 * (iota(2 * row_count) % 2)).astype(jnp.float32)
     values = 2.0 * values + alternating[:, None] * nyquist[None, :]
     out_scale = 1.0 / (length * math.sqrt(length // 2))

time: 394 us -> 385 us (0.977)
  other arithmetic: 33.6 us -> 22.4 us
  local copies, waits for them, and re-layouts: 39.9 us -> 48.8 us
  waiting for transfers between devices: 91 us -> 83.6 us
    add x4 -> x6, other arithmetic: 20.9 us -> 5.97 us  [rotate(): real_part * sine + imag_part * cosine]
    unnamed x40 -> x80, local copies, waits for them, and re-layouts: 0.83 us -> 12.5 us
    all_to_all x5 -> x6, waiting for transfers between devices: 52.2 us -> 44.4 us  [local(): got = lax.all_to_all(payload, 'fft', 0, 0, tiled=True)]
    sin x2 -> x7, other arithmetic: 0.22 us -> 5.03 us  [the longest x1 4.22 us: local(): jnp.sin(big_angle)]
    squeeze x4 -> x1, local copies, waits for them, and re-layouts: 4.87 us -> 0.08 us  [local(): full_imag = got[:, 1]]
    dot_general x74 -> x88, matrix products: 169 us -> 170 us  [contract(): jnp.einsum(pattern, left_op, right_op, precision=exact_precision, preferr...]
    all_to_all x5 -> x6, starting transfers between devices: 34.9 us -> 35.1 us  [local(): got = lax.all_to_all(payload, 'fft', 0, 0, tiled=True)]
  transfers between devices with their start and end apart: 9 -> 10, of which waited for: 8 -> 10; matrix products, arithmetic and copies ran while one was open for 30% -> 32% of each run, Pallas kernels for 0% -> 0%
where the time goes in v3:
time: 385 us; the launch traced here: 378 us
  matrix products  170 us (44%)
  waiting for transfers between devices  83.6 us (22%)
  starting transfers between devices  52.1 us (14%)
  local copies, waits for them, and re-layouts  48.8 us (13%)
  other arithmetic  22.4 us (6%)
    dot_general x88, matrix products, contract(): jnp.einsum(pattern, left_op, right_op, precision=exact_precision, preferr...  170 us
    all_to_all x6, waiting for transfers between devices, local(): got = lax.all_to_all(payload, 'fft', 0, 0, tiled=True)  44.4 us
    all_to_all x4, waiting for transfers between devices, local(): arrived = lax.all_to_all(outgoing, 'entry', 0, 0, tiled=True)  39.2 us
    all_to_all x6, starting transfers between devices, local(): got = lax.all_to_all(payload, 'fft', 0, 0, tiled=True)  35.1 us
    all_to_all x4, starting transfers between devices, local(): arrived = lax.all_to_all(outgoing, 'entry', 0, 0, tiled=True)  17 us
    unnamed x80, local copies, waits for them, and re-layouts  12.5 us
    another operation x4, local copies, waits for them, and re-layouts, local(): payload = jnp.stack([half_real, half_imag], axis=1)  10.3 us
  transfers between devices with their start and end apart: 10, of which 10 were waited for; matrix products, arithmetic and copies ran while one was open for 32% of the time, Pallas kernels for 0%

profile of v3, /device:TPU:0, one launch (start us, length us, event | category | flops | bytes accessed | tf_op | source)
XLA Modules:
  0.0 378.1 jit_solution(2178451484130153110)
XLA Ops:
  0.0 2.3 fusion.139
  2.3 4.7 %all-to-all-start.6 = ((f32[4,512,128]{2,1,0:T(8,128)}), f32[4,512,128]{2,1,0:T(8,128)S(1)}, u32[]{:S(2)}, u32[]{:S(2)}) async-start(f32[4,512,128]{2,1,0:T(8,128)} %fusion.139), calls=%async_computation.6 | async-start | bytes 2097152 | tf_op jit(solution)/shard_map/all_to_all | solution.py:168
  8.2 14.8 %all-to-all-done.6 = f32[4,512,128]{2,1,0:T(8,128)S(1)} async-done(((f32[4,512,128]{2,1,0:T(8,128)}), f32[4,512,128]{2,1,0:T(8,128)S(1)}, u32[]{:S(2)}, u32[]{:S(2)}) %all-to-all-start.6) | async-done | bytes 1048608 | tf_op jit(solution)/shard_map/all_to_all | solution.py:168
  23.0 3.5 all-to-all-start.4
  29.2 13.2 %all-to-all-done.4 = f32[4,512,128]{2,1,0:T(8,128)S(1)} async-done(((f32[4,512,128]{2,1,0:T(8,128)}), f32[4,512,128]{2,1,0:T(8,128)S(1)}, u32[]{:S(2)}, u32[]{:S(2)}) %all-to-all-start.4) | async-done | bytes 1048608 | tf_op jit(solution)/shard_map/all_to_all | solution.py:168
  42.4 4.3 %all-to-all-start = ((f32[4,512,128]{2,1,0:T(8,128)}), f32[4,512,128]{2,1,0:T(8,128)}, u32[]{:S(2)}, u32[]{:S(2)}) async-start(f32[4,512,128]{2,1,0:T(8,128)} %fusion.133), calls=%async_computation | async-start | bytes 2097152 | tf_op jit(solution)/shard_map/all_to_all | solution.py:168
  46.9 3.1 fusion.116
  50.0 3.2 fusion.118
  53.3 3.2 fusion.120
  56.4 6.2 %all-to-all-done = f32[4,512,128]{2,1,0:T(8,128)} async-done(((f32[4,512,128]{2,1,0:T(8,128)}), f32[4,512,128]{2,1,0:T(8,128)}, u32[]{:S(2)}, u32[]{:S(2)}) %all-to-all-start) | async-done | bytes 1048608 | tf_op jit(solution)/shard_map/all_to_all | solution.py:168
  62.7 4.5 %all-to-all-start.2 = ((f32[4,512,128]{2,1,0:T(8,128)}), f32[4,512,128]{2,1,0:T(8,128)}, u32[]{:S(2)}, u32[]{:S(2)}) async-start(f32[4,512,128]{2,1,0:T(8,128)} %fusion.135), calls=%async_computation.2 | async-start | bytes 2097152 | tf_op jit(solution)/shard_map/all_to_all | solution.py:168
  68.6 3.1 fusion.122
  71.8 3.2 fusion.128
  74.9 3.3 fusion.130
  78.2 5.0 %all-to-all-done.2 = f32[4,512,128]{2,1,0:T(8,128)} async-done(((f32[4,512,128]{2,1,0:T(8,128)}), f32[4,512,128]{2,1,0:T(8,128)}, u32[]{:S(2)}, u32[]{:S(2)}) %all-to-all-start.2) | async-done | bytes 1048608 | tf_op jit(solution)/shard_map/all_to_all | solution.py:168
  86.5 9.4 %multiply_add_fusion.2 = (f32[64,64,128]{2,0,1:T(8,128)}, f32[64,64,128]{2,0,1:T(8,128)}, f32[64,64,128]{2,0,1:T(8,128)}, f32[64,64,128]{2,0,1:T(8,128)}, f32[64...) fusion(f32[64,64,128]{2,0,1:T(8,128)S(1)} %fusion.126, ...), kind=kOutput, calls=%fused_computation.19 | convolution fusion | flops 213909504 | bytes 32546816 | tf_op jit(solution)/shard_map/ja,an->jn/dot_general | solution.py:15
  95.9 2.3 fusion.1
  98.3 2.3 fusion.3
  100.6 2.3 fusion.78
  103.1 3.3 fusion.72
  107.8 2.5 copy.167
  110.3 8.6 %all-to-all-start.7 = ((f32[32,2,64,128]{3,2,1,0:T(8,128)}), f32[32,2,64,128]{3,2,1,0:T(8,128)}, u32[]{:S(2)}, u32[]{:S(2)}) async-start(f32[32,2,64,128]{3,2,1,0:T(8,128)} %copy.167), calls=%async_computation.7 | async-start | bytes 4194304 | tf_op jit(solution)/shard_map/all_to_all | solution.py:172
  119.4 4.2 %fusion.150 = (f32[32,65,128]{2,0,1:T(8,128)S(1)}, f32[32,65,128]{2,0,1:T(8,128)S(1)}) fusion(s32[65]{0:T(128)S(1)} %pad_add_fusion, s32[32,128]{1,0:T(8,128)S(1)} %iota_add_fusion), kind=kLoop, calls=%fused_computation.225 | loop fusion | flops 3727360 | bytes 2146564 | tf_op jit(solution)/shard_map/sin | solution.py:159
  123.8 3.9 %fusion.9 = f32[32,64,128]{2,0,1:T(8,128)S(1)} fusion(f32[64,64,128]{2,0,1:T(8,128)} %get-tuple-element.150, f32[32,64]{1,0:T(8,128)S(1)} %get-tuple-element.128), kind=kOutput, calls=%fused_computation.34 | convolution fusion | flops 201326592 | bytes 3153920 | tf_op jit(solution)/shard_map/mb,jbc->mjc/dot_general | solution.py:15
  127.7 3.3 fusion.66
  132.2 4.0 %fusion.11 = f32[32,64,128]{2,0,1:T(8,128)S(1)} fusion(f32[64,64,128]{2,0,1:T(8,128)} %get-tuple-element.150, f32[32,64]{1,0:T(8,128)S(1)} %get-tuple-element.134), kind=kOutput, calls=%fused_computation.36 | convolution fusion | flops 201326592 | bytes 3153920 | tf_op jit(solution)/shard_map/mb,jbc->mjc/dot_general | solution.py:15
  136.3 2.4 fusion.60
  138.9 2.7 copy.155
  141.5 5.2 %all-to-all-done.7 = f32[32,2,64,128]{3,2,1,0:T(8,128)} async-done(((f32[32,2,64,128]{3,2,1,0:T(8,128)}), f32[32,2,64,128]{3,2,1,0:T(8,128)}, u32[]{:S(2)}, u32[]{:S(2)}) %all-to-all-start.7) | async-done | bytes 2097184 | tf_op jit(solution)/shard_map/all_to_all | solution.py:172
  146.8 5.4 %all-to-all-start.5 = ((f32[32,2,64,128]{3,2,1,0:T(8,128)}), f32[32,2,64,128]{3,2,1,0:T(8,128)}, u32[]{:S(2)}, u32[]{:S(2)}) async-start(f32[32,2,64,128]{3,2,1,0:T(8,128)} %copy.155), calls=%async_computation.5 | async-start | bytes 4194304 | tf_op jit(solution)/shard_map/all_to_all | solution.py:172
  155.6 4.0 %fusion.25 = f32[32,64,128]{2,0,1:T(8,128)S(1)} fusion(f32[64,64,128]{2,0,1:T(8,128)} %get-tuple-element.135, f32[32,64]{1,0:T(8,128)S(1)} %get-tuple-element.128), kind=kOutput, calls=%fused_computation.50 | convolution fusion | flops 201326592 | bytes 3153920 | tf_op jit(solution)/shard_map/mb,jbc->mjc/dot_general | solution.py:15
  159.7 3.3 fusion.42
  164.3 4.0 %fusion.27 = f32[32,64,128]{2,0,1:T(8,128)S(1)} fusion(f32[64,64,128]{2,0,1:T(8,128)} %get-tuple-element.135, f32[32,64]{1,0:T(8,128)S(1)} %get-tuple-element.134), kind=kOutput, calls=%fused_computation.52 | convolution fusion | flops 201326592 | bytes 3153920 | tf_op jit(solution)/shard_map/mb,jbc->mjc/dot_general | solution.py:15
  168.3 2.4 fusion.36
  170.9 2.5 copy.127
  174.4 2.3 fusion.17
  176.8 3.5 all-to-all-done.5
  180.2 5.1 %all-to-all-start.1 = ((f32[32,2,64,128]{3,2,1,0:T(8,128)}), f32[32,2,64,128]{3,2,1,0:T(8,128)}, u32[]{:S(2)}, u32[]{:S(2)}) async-start(f32[32,2,64,128]{3,2,1,0:T(8,128)} %copy.127), calls=%async_computation.1 | async-start | bytes 4194304 | tf_op jit(solution)/shard_map/all_to_all | solution.py:172
  185.5 4.9 %fusion.54 = f32[32,1,64,128]{3,0,2,1:T(8,128)} fusion(f32[32,64,128]{2,0,1:T(8,128)S(1)} %fusion.17, f32[64,64,128]{2,0,1:T(8,128)} %get-tuple-element.145, f32[32,64]{1,0:T(8,128)S(1)} %get-tuple-element.134), kind=kOutput, calls=%fused_computation.83 | convolution fusion | flops 201588736 | bytes 4202496 | tf_op jit(solution)/shard_map/mb,jbc->mjc/dot_general | solution.py:15
  191.6 4.0 %fusion.19 = f32[32,64,128]{2,0,1:T(8,128)S(1)} fusion(f32[64,64,128]{2,0,1:T(8,128)} %get-tuple-element.146, f32[32,64]{1,0:T(8,128)S(1)} %get-tuple-element.134), kind=kOutput, calls=%fused_computation.44 | convolution fusion | flops 201326592 | bytes 3153920 | tf_op jit(solution)/shard_map/mb,jbc->mjc/dot_general | solution.py:15
  195.7 2.4 fusion.48
  198.3 2.5 copy.139
  211.3 2.5 all-to-all-done.1
  213.8 6.5 %all-to-all-start.3 = ((f32[32,2,64,128]{3,2,1,0:T(8,128)}), f32[32,2,64,128]{3,2,1,0:T(8,128)}, u32[]{:S(2)}, u32[]{:S(2)}) async-start(f32[32,2,64,128]{3,2,1,0:T(8,128)} %copy.139), calls=%async_computation.3 | async-start | bytes 4194304 | tf_op jit(solution)/shard_map/all_to_all | solution.py:172
  228.9 2.0 fusion.294
  230.9 2.0 fusion.257
  232.9 2.1 fusion.297
  235.0 2.1 fusion.260
  237.2 2.0 fusion.303
  239.2 2.0 fusion.266
  241.2 6.6 %all-to-all-done.3 = f32[32,2,64,128]{3,2,1,0:T(8,128)} async-done(((f32[32,2,64,128]{3,2,1,0:T(8,128)}), f32[32,2,64,128]{3,2,1,0:T(8,128)}, u32[]{:S(2)}, u32[]{:S(2)}) %all-to-all-start.3) | async-done | bytes 2097184 | tf_op jit(solution)/shard_map/all_to_all | solution.py:172
  262.7 2.8 multiply_add_fusion.8
  265.5 2.0 fusion.99
  278.0 2.2 fusion.93
  292.9 2.4 add_add_fusion
  308.9 4.8 %all-to-all-start.8 = ((f32[32,2,32,128]{3,2,1,0:T(8,128)}), f32[32,2,32,128]{3,2,1,0:T(8,128)S(1)}, u32[]{:S(2)}, u32[]{:S(2)}) async-start(f32[32,2,32,128]{3,2,1,0:T(8,128)} %copy.180), calls=%async_computation.8 | async-start | bytes 2097152 | tf_op jit(solution)/shard_map/all_to_all | solution.py:214
  316.2 14.5 %all-to-all-done.8 = f32[32,2,32,128]{3,2,1,0:T(8,128)S(1)} async-done(((f32[32,2,32,128]{3,2,1,0:T(8,128)}), f32[32,2,32,128]{3,2,1,0:T(8,128)S(1)}, u32[]{:S(2)}, u32[]{:S(2)}) %all-to-all-start.8) | async-done | bytes 1048608 | tf_op jit(solution)/shard_map/all_to_all | solution.py:214
  330.7 4.7 %all-to-all-start.9 = ((f32[32,2,32,128]{3,2,1,0:T(8,128)}), f32[32,2,32,128]{3,2,1,0:T(8,128)}, u32[]{:S(2)}, u32[]{:S(2)}) async-start(f32[32,2,32,128]{3,2,1,0:T(8,128)} %copy.187), calls=%async_computation.9 | async-start | bytes 2097152 | tf_op jit(solution)/shard_map/all_to_all | solution.py:214
  335.5 2.2 fusion.162
  338.9 12.2 %all-to-all-done.9 = f32[32,2,32,128]{3,2,1,0:T(8,128)} async-done(((f32[32,2,32,128]{3,2,1,0:T(8,128)}), f32[32,2,32,128]{3,2,1,0:T(8,128)}, u32[]{:S(2)}, u32[]{:S(2)}) %all-to-all-start.9) | async-done | bytes 1048608 | tf_op jit(solution)/shard_map/all_to_all | solution.py:214
  352.4 2.2 fusion.156
  354.6 2.2 fusion.154
  357.3 2.5 fusion.81
  372.8 2.3 add_multiply_fusion
  (213 shorter events, 111.4 us)
Async XLA Ops:
  2.3 4.8 %copy-start.24 = (s32[512,128]{1,0:T(8,128)S(1)}, s32[512,128]{1,0:T(8,128)}, u32[]{:S(2)}) copy-start(s32[512,128]{1,0:T(8,128)} %param.23) | copy-start | bytes 786436
  2.3 4.8 %copy-start.25 = (s32[512,128]{1,0:T(8,128)S(1)}, s32[512,128]{1,0:T(8,128)}, u32[]{:S(2)}) copy-start(s32[512,128]{1,0:T(8,128)} %param.21) | copy-start | bytes 786436
  2.3 20.6 %all-to-all-start.6 = ((f32[4,512,128]{2,1,0:T(8,128)}), f32[4,512,128]{2,1,0:T(8,128)S(1)}, u32[]{:S(2)}, u32[]{:S(2)}) async-start(f32[4,512,128]{2,1,0:T(8,128)} %fusion.139), calls=%async_computation.6 | async-start | bytes 2097152 | tf_op jit(solution)/shard_map/all_to_all | solution.py:168
  8.2 18.7 %copy-start.26 = (s32[512,128]{1,0:T(8,128)S(1)}, s32[512,128]{1,0:T(8,128)}, u32[]{:S(2)}) copy-start(s32[512,128]{1,0:T(8,128)} %param.25) | copy-start | bytes 786436
  8.2 18.7 %copy-start.27 = (s32[512,128]{1,0:T(8,128)S(1)}, s32[512,128]{1,0:T(8,128)}, u32[]{:S(2)}) copy-start(s32[512,128]{1,0:T(8,128)} %param.24) | copy-start | bytes 786436
  23.0 19.4 %all-to-all-start.4 = ((f32[4,512,128]{2,1,0:T(8,128)}), f32[4,512,128]{2,1,0:T(8,128)S(1)}, u32[]{:S(2)}, u32[]{:S(2)}) async-start(f32[4,512,128]{2,1,0:T(8,128)} %fusion.137), calls=%async_computation.4 | async-start | bytes 2097152 | tf_op jit(solution)/shard_map/all_to_all | solution.py:168
  26.5 1.5 copy-start.28
  26.5 1.4 copy-start.29
  42.4 20.3 %all-to-all-start = ((f32[4,512,128]{2,1,0:T(8,128)}), f32[4,512,128]{2,1,0:T(8,128)}, u32[]{:S(2)}, u32[]{:S(2)}) async-start(f32[4,512,128]{2,1,0:T(8,128)} %fusion.133), calls=%async_computation | async-start | bytes 2097152 | tf_op jit(solution)/shard_map/all_to_all | solution.py:168
  62.7 20.5 %all-to-all-start.2 = ((f32[4,512,128]{2,1,0:T(8,128)}), f32[4,512,128]{2,1,0:T(8,128)}, u32[]{:S(2)}, u32[]{:S(2)}) async-start(f32[4,512,128]{2,1,0:T(8,128)} %fusion.135), calls=%async_computation.2 | async-start | bytes 2097152 | tf_op jit(solution)/shard_map/all_to_all | solution.py:168
  84.6 1.9 copy-start.8
  110.3 36.4 %all-to-all-start.7 = ((f32[32,2,64,128]{3,2,1,0:T(8,128)}), f32[32,2,64,128]{3,2,1,0:T(8,128)}, u32[]{:S(2)}, u32[]{:S(2)}) async-start(f32[32,2,64,128]{3,2,1,0:T(8,128)} %copy.167), calls=%async_computation.7 | async-start | bytes 4194304 | tf_op jit(solution)/shard_map/all_to_all | solution.py:172
  118.9 4.7 %copy-start.3 = (f32[64,64,128]{2,0,1:T(8,128)S(1)}, f32[64,64,128]{2,0,1:T(8,128)}, u32[]{:S(2)}) copy-start(f32[64,64,128]{2,0,1:T(8,128)} %get-tuple-element.149) | copy-start | bytes 6291460
  132.2 4.0 %copy-start.4 = (f32[64,64,128]{2,0,1:T(8,128)S(1)}, f32[64,64,128]{2,0,1:T(8,128)}, u32[]{:S(2)}) copy-start(f32[64,64,128]{2,0,1:T(8,128)} %get-tuple-element.149) | copy-start | bytes 6291460
  136.3 2.4 copy-start.19
  146.8 33.5 %all-to-all-start.5 = ((f32[32,2,64,128]{3,2,1,0:T(8,128)}), f32[32,2,64,128]{3,2,1,0:T(8,128)}, u32[]{:S(2)}, u32[]{:S(2)}) async-start(f32[32,2,64,128]{3,2,1,0:T(8,128)} %copy.155), calls=%async_computation.5 | async-start | bytes 4194304 | tf_op jit(solution)/shard_map/all_to_all | solution.py:172
  155.6 4.0 %copy-start.1 = (f32[64,64,128]{2,0,1:T(8,128)S(1)}, f32[64,64,128]{2,0,1:T(8,128)}, u32[]{:S(2)}) copy-start(f32[64,64,128]{2,0,1:T(8,128)} %get-tuple-element.133) | copy-start | bytes 6291460
  164.3 4.0 %copy-start.2 = (f32[64,64,128]{2,0,1:T(8,128)S(1)}, f32[64,64,128]{2,0,1:T(8,128)}, u32[]{:S(2)}) copy-start(f32[64,64,128]{2,0,1:T(8,128)} %get-tuple-element.133) | copy-start | bytes 6291460
  168.3 2.4 copy-start.20
  170.9 3.5 copy-start.5
  180.2 33.6 %all-to-all-start.1 = ((f32[32,2,64,128]{3,2,1,0:T(8,128)}), f32[32,2,64,128]{3,2,1,0:T(8,128)}, u32[]{:S(2)}, u32[]{:S(2)}) async-start(f32[32,2,64,128]{3,2,1,0:T(8,128)} %copy.127), calls=%async_computation.1 | async-start | bytes 4194304 | tf_op jit(solution)/shard_map/all_to_all | solution.py:172
  191.6 4.0 %copy-start = (f32[64,64,128]{2,0,1:T(8,128)S(1)}, f32[64,64,128]{2,0,1:T(8,128)}, u32[]{:S(2)}) copy-start(f32[64,64,128]{2,0,1:T(8,128)} %get-tuple-element.145) | copy-start | bytes 6291460
  195.6 2.4 copy-start.21
  213.8 33.9 %all-to-all-start.3 = ((f32[32,2,64,128]{3,2,1,0:T(8,128)}), f32[32,2,64,128]{3,2,1,0:T(8,128)}, u32[]{:S(2)}, u32[]{:S(2)}) async-start(f32[32,2,64,128]{3,2,1,0:T(8,128)} %copy.139), calls=%async_computation.3 | async-start | bytes 4194304 | tf_op jit(solution)/shard_map/all_to_all | solution.py:172
  222.1 1.2 copy-start.15
  222.1 1.5 copy-start.22
  222.1 1.5 copy-start.30
  223.6 1.2 copy-start.16
  223.6 1.5 copy-start.23
  252.5 1.2 copy-start.14
  253.8 1.2 copy-start.12
  255.0 1.2 copy-start.6
  255.0 1.5 copy-start.13
  256.5 1.2 copy-start.10
  257.8 1.2 copy-start.7
  257.8 1.5 copy-start.11
  259.3 1.2 copy-start.9
  261.6 1.1 copy-start.33
  305.7 0.7 copy-start.31
  305.7 0.7 copy-start.32
  308.9 21.7 %all-to-all-start.8 = ((f32[32,2,32,128]{3,2,1,0:T(8,128)}), f32[32,2,32,128]{3,2,1,0:T(8,128)S(1)}, u32[]{:S(2)}, u32[]{:S(2)}) async-start(f32[32,2,32,128]{3,2,1,0:T(8,128)} %copy.180), calls=%async_computation.8 | async-start | bytes 2097152 | tf_op jit(solution)/shard_map/all_to_all | solution.py:214
  330.7 20.5 %all-to-all-start.9 = ((f32[32,2,32,128]{3,2,1,0:T(8,128)}), f32[32,2,32,128]{3,2,1,0:T(8,128)}, u32[]{:S(2)}, u32[]{:S(2)}) async-start(f32[32,2,32,128]{3,2,1,0:T(8,128)} %copy.187), calls=%async_computation.9 | async-start | bytes 2097152 | tf_op jit(solution)/shard_map/all_to_all | solution.py:214
  364.1 1.9 copy-start.18
  367.2 1.2 copy-start.17
